TPU v7x, 128 devices: a whole 4x4x4 slice. The times are simulated.
128 devices in a mesh: group: 4 (over y), local: 32 (over x, z, core).
Axes of the slice: x: 4, y: 4, z: 4, core: 2. Of those that a mesh axis runs over, the one named last changes fastest.
Arguments:
- tokens: bfloat16 [16384, 3584], P(('group', 'local')), may hold values from -6 to 6
- grad_out: bfloat16 [16384, 3584], P(('group', 'local')), may hold values from -6 to 6
- expert_ids: int32 [16384, 4], P(('group', 'local')), may hold values from 0 to 127, as said below
- combine: bfloat16 [16384, 4], P(('group', 'local')), may hold values from 0.099609375 to 1
- gate_weight: bfloat16 [128, 3584, 1024], P(('group', 'local')), may hold values from -0.09375 to 0.09375
- up_weight: bfloat16 [128, 3584, 1024], P(('group', 'local')), may hold values from -0.09375 to 0.09375
- down_weight: bfloat16 [128, 1024, 3584], P(('group', 'local')), may hold values from -0.1875 to 0.1875
Outputs:
- grad_tokens: bfloat16 [16384, 3584], P(('group', 'local'))
- grad_combine: bfloat16 [16384, 4], P(('group', 'local'))
Inputs may be any that keep to these rules, and one draw needn't show every extreme that they name: `expert_ids`: each token names 4 different experts; expert e lies in node group e // 32. The first 2 experts of a token lie in one group and the other 2 in another, so a token uses 2 groups. The tokens of each device choose every group exactly 128//2 times. The tokens of one device name one expert at most 6 times, and in every draw some expert is named 6 times by the tokens of every device.
All inputs are finite; a program needn't handle non-finite values.
Results may differ from a plain program's by a relative error of at most 0.0058.
Values may be sent and summed in bfloat16 or wider, within the bound.
No kernel may reach another device: no remote copies, remote signals or barrier semaphores. Data moves between devices by JAX's collectives and lax.ppermute only.
A program may use at most 128 MiB of HBM per device.

v0:
```python
import jax
import jax.numpy as jnp
from jax import lax
from jax.sharding import PartitionSpec as P


def _t_dot(a, b):
    return lax.dot_general(a, b, (((1,), (1,)), ((), ())), preferred_element_type=jnp.float32)


def local(tokens, grad_out, expert_ids, combine, gate_weight, up_weight, down_weight):
    token_rows, model_width = tokens.shape
    top_count = expert_ids.shape[1]
    group_count = lax.axis_size("group")
    local_count = lax.axis_size("local")
    expert_count = group_count * local_count
    mean_pair = token_rows * top_count // expert_count
    pair_cap = mean_pair + (mean_pair + 1) // 2
    slot_cap = pair_cap
    gate_mat = gate_weight[0]
    up_mat = up_weight[0]
    down_mat = down_weight[0]
    ff = gate_mat.shape[1]
    assign_count = token_rows * top_count
    lane = 128
    targets = expert_ids.reshape(assign_count)
    one_hot = (targets[:, None] == jnp.arange(expert_count, dtype=jnp.int32)[None, :]).astype(
        jnp.int32
    )
    rank_in = jnp.sum((jnp.cumsum(one_hot, axis=0) - 1) * one_hot, axis=1)
    slot_of = targets * slot_cap + rank_in
    slot_total = expert_count * slot_cap
    sel = slot_of[None, :] == jnp.arange(slot_total, dtype=jnp.int32)[:, None]
    sel_a = sel.astype(jnp.bfloat16)
    sel_t = jnp.any(sel.reshape(slot_total, token_rows, top_count), axis=2).astype(jnp.bfloat16)

    send_x = jnp.dot(sel_t, tokens, preferred_element_type=jnp.bfloat16)
    cols = jnp.arange(lane, dtype=jnp.int32)[None, :]
    info = jnp.zeros((token_rows, lane), jnp.bfloat16)
    for k in range(top_count):
        info = jnp.where(cols == k, combine[:, k : k + 1], info)
        info = jnp.where(cols == top_count + k, expert_ids[:, k : k + 1].astype(jnp.bfloat16), info)
    send_dyp = jnp.dot(
        sel_t, jnp.concatenate([grad_out, info], axis=1), preferred_element_type=jnp.bfloat16
    )

    def a2a(v):
        width = v.shape[-1]
        v = v.reshape(expert_count, slot_cap * width // lane, lane)
        v = lax.all_to_all(v, ("group", "local"), split_axis=0, concat_axis=0, tiled=True)
        return v.reshape(slot_total, width)

    rows_x = a2a(send_x)
    gate_pre = jnp.dot(rows_x, gate_mat, preferred_element_type=jnp.float32)
    up_pre = jnp.dot(rows_x, up_mat, preferred_element_type=jnp.float32)
    sigmoid_gate = jax.nn.sigmoid(gate_pre)
    active = gate_pre * sigmoid_gate
    hidden = (active * up_pre).astype(jnp.bfloat16)
    output = jnp.dot(hidden, down_mat, preferred_element_type=jnp.float32)
    gate_factor = up_pre * sigmoid_gate * (1.0 + gate_pre * (1.0 - sigmoid_gate))
    gate_factor, active, output = lax.optimization_barrier((gate_factor, active, output))

    rows_dyp = a2a(send_dyp)
    rows_dy = rows_dyp[:, :model_width]
    e_me = (lax.axis_index("group") * local_count + lax.axis_index("local")).astype(jnp.float32)
    info_rows = rows_dyp[:, model_width : model_width + 2 * top_count].astype(jnp.float32)
    rows_p = jnp.sum(
        jnp.where(info_rows[:, top_count:] == e_me, info_rows[:, :top_count], 0.0), axis=1
    )
    back_hidden = _t_dot(rows_dy, down_mat)
    back_hidden = back_hidden * rows_p[:, None]
    grad_gate = (back_hidden * gate_factor).astype(jnp.bfloat16)
    grad_up = (back_hidden * active).astype(jnp.bfloat16)

    half = model_width // 2
    contrib_a = (_t_dot(grad_gate, gate_mat[:half]) + _t_dot(grad_up, up_mat[:half])).astype(
        jnp.bfloat16
    )
    back_a = a2a(contrib_a)
    contrib_b = (_t_dot(grad_gate, gate_mat[half:]) + _t_dot(grad_up, up_mat[half:])).astype(
        jnp.bfloat16
    )
    grad_weight = jnp.sum(rows_dy.astype(jnp.float32) * output, axis=1).astype(jnp.bfloat16)
    gw_block = jnp.zeros((slot_total, lane), jnp.bfloat16).at[:, 0].set(grad_weight)
    back_b = a2a(jnp.concatenate([contrib_b, gw_block], axis=1))

    sum_a = jnp.dot(sel_t.T, back_a, preferred_element_type=jnp.float32)
    sum_b = jnp.dot(sel_t.T, back_b[:, : model_width - half], preferred_element_type=jnp.float32)
    grad_tokens = jnp.concatenate([sum_a, sum_b], axis=1).astype(jnp.bfloat16)
    gw_back = jnp.dot(sel_a.T, back_b[:, model_width - half :], preferred_element_type=jnp.float32)
    grad_combine = gw_back[:, 0].astype(jnp.bfloat16).reshape(token_rows, top_count)
    return (grad_tokens, grad_combine)


def solution(mesh):
    placed = (
        P(("group", "local"), None),
        P(("group", "local"), None),
        P(("group", "local"), None),
        P(("group", "local"), None),
        P(("group", "local"), None, None),
        P(("group", "local"), None, None),
        P(("group", "local"), None, None),
    )
    return jax.shard_map(
        local,
        mesh=mesh,
        in_specs=placed,
        out_specs=(P(("group", "local"), None), P(("group", "local"), None)),
        check_vma=False,
    )
```

profile of v0, /device:TPU:1, one launch (start us, length us, event | category | flops | bytes accessed | tf_op | source)
XLA Modules:
  0.0 325.8 jit_solution(17960901231254734133)
XLA Ops:
  0.6 0.0 copy-start
  0.6 0.9 copy.28
  1.5 0.1 eq.143
  1.6 0.1 eq.139
  1.7 0.1 copy.30
  1.8 0.2 fusion.42
  2.1 0.1 add_add_fusion
  2.2 0.2 fusion.41
  2.4 0.1 reduce_sum.30
  2.5 0.1 copy.32
  2.6 0.8 fusion.49
  3.4 0.2 fusion.33
  3.6 0.0 copy-done
  3.6 4.0 %fusion.50 = bf16[768,3584]{1,0:T(8,128)(2,1)} fusion(pred[768,128]{1,0:T(8,128)(4,1)S(1)} %fusion.33, bf16[128,3584]{1,0:T(8,128)(2,1)S(1)} %copy-done), kind=kOutput, calls=%fused_computation.86 | convolution fusion | flops 704643072 | bytes 6520832 | tf_op jit(solution)/shard_map/dot_general | solution.py:37
  7.6 11.1 %reshape.156 = bf16[128,168,128]{2,1,0:T(8,128)(2,1)} reshape(bf16[768,3584]{1,0:T(8,128)(2,1)} %fusion.50) | data formatting | bytes 11010048 | tf_op jit(solution)/shard_map/reshape | solution.py:49
  18.7 11.9 %all-to-all-start.1 = ((bf16[128,168,128]{2,1,0:T(8,128)(2,1)}), bf16[128,168,128]{2,1,0:T(8,128)(2,1)}, u32[]{:S(2)}, u32[]{:S(2)}) async-start(bf16[128,168,128]{2,1,0:T(8,128)(2,1)} %reshape.156), calls=%async_computation.1 | async-start | bytes 11010048 | tf_op jit(solution)/shard_map/all_to_all | solution.py:50
  30.7 0.0 copy-done.4
  30.7 0.2 select_select_fusion
  30.9 0.0 copy-done.3
  30.9 4.1 %fusion.35 = bf16[768,3712]{1,0:T(8,128)(2,1)} fusion(pred[768,128]{1,0:T(8,128)(4,1)S(1)} %fusion.33, bf16[128,128]{1,0:T(8,128)(2,1)S(1)} %select_select_fusion, bf16[128,3584]{1,0:T(8,128)(2,1)S(1)} %copy-done.3), kind=kOutput, calls=%fused_computation.41 | convolution fusion | flops 731709440 | bytes 6750208 | tf_op jit(solution)/shard_map/dot_general | solution.py:43
  35.0 11.9 %reshape.154 = bf16[128,174,128]{2,1,0:T(8,128)(2,1)} reshape(bf16[768,3712]{1,0:T(8,128)(2,1)} %fusion.35) | data formatting | bytes 11403264 | tf_op jit(solution)/shard_map/reshape | solution.py:49
  46.9 52.2 %all-to-all-done.1 = bf16[128,168,128]{2,1,0:T(8,128)(2,1)} async-done(((bf16[128,168,128]{2,1,0:T(8,128)(2,1)}), bf16[128,168,128]{2,1,0:T(8,128)(2,1)}, u32[]{:S(2)}, u32[]{:S(2)}) %all-to-all-start.1) | async-done | bytes 5505056 | tf_op jit(solution)/shard_map/all_to_all | solution.py:50
  99.1 7.8 %all-to-all-start = ((bf16[128,174,128]{2,1,0:T(8,128)(2,1)}), bf16[128,174,128]{2,1,0:T(8,128)(2,1)}, u32[]{:S(2)}, u32[]{:S(2)}) async-start(bf16[128,174,128]{2,1,0:T(8,128)(2,1)} %reshape.154), calls=%async_computation | async-start | bytes 11534336 | tf_op jit(solution)/shard_map/all_to_all | solution.py:50
  106.9 0.6 compare_reduce_fusion
  107.6 10.6 %reshape.157 = bf16[768,3584]{1,0:T(8,128)(2,1)} reshape(bf16[128,168,128]{2,1,0:T(8,128)(2,1)} %all-to-all-done.1) | data formatting | bytes 11010048 | tf_op jit(solution)/shard_map/reshape | solution.py:51
  118.2 9.8 %fusion.2 = f32[768,1024]{1,0:T(8,128)S(1)} fusion(bf16[768,3584]{1,0:T(8,128)(2,1)} %reshape.157, bf16[1,3584,1024]{2,1,0:T(8,128)(2,1)} %param.14), kind=kOutput, calls=%fused_computation.3 | convolution fusion | flops 5637144576 | bytes 15990784 | tf_op jit(solution)/shard_map/dot_general | solution.py:55
  128.0 0.0 copy-done.2
  128.0 0.0 slice-start.1
  128.1 10.9 %fusion.26 = (f32[768,1024]{1,0:T(8,128)}, f32[768,1024]{1,0:T(8,128)}, f32[768,1024]{1,0:T(8,128)S(1)}) fusion(f32[768,1024]{1,0:T(8,128)S(1)} %fusion.2, bf16[768,3584]{1,0:T(8,128)(2,1)S(1)} %copy-done.2, bf16[1,3584,1024]{2,1,0:T(8,128)(2,1)} %param.13), kind=kOutput, calls=%fused_computation.31 | convolution fusion | flops 5644222464 | bytes 25427968 | tf_op jit(solution)/shard_map/dot_general | solution.py:54
  139.0 0.0 slice-done
  139.0 0.0 slice-done.1
  139.0 9.5 %fusion.4 = f32[768,3584]{1,0:T(8,128)} fusion(bf16[1,1024,3584]{2,1,0:T(8,128)(2,1)S(1)} %bitcast.68, f32[768,1024]{1,0:T(8,128)S(1)} %fusion.2, f32[768,1024]{1,0:T(8,128)S(1)} %get-tuple-element.42), kind=kOutput, calls=%fused_computation.5 | convolution fusion | flops 5641863168 | bytes 24641536 | tf_op jit(solution)/shard_map/dot_general | solution.py:59
  148.5 29.0 %all-to-all-done = bf16[128,174,128]{2,1,0:T(8,128)(2,1)} async-done(((bf16[128,174,128]{2,1,0:T(8,128)(2,1)}), bf16[128,174,128]{2,1,0:T(8,128)(2,1)}, u32[]{:S(2)}, u32[]{:S(2)}) %all-to-all-start) | async-done | bytes 5701664 | tf_op jit(solution)/shard_map/all_to_all | solution.py:50
  177.4 11.5 %reshape.155 = bf16[768,3712]{1,0:T(8,128)(2,1)} reshape(bf16[128,174,128]{2,1,0:T(8,128)(2,1)} %all-to-all-done) | data formatting | bytes 11403264 | tf_op jit(solution)/shard_map/reshape | solution.py:51
  189.0 1.0 slice_convert_fusion
  189.9 0.3 fusion.40
  190.2 11.4 %multiply_convert_fusion.1 = (bf16[768,1024]{1,0:T(8,128)(2,1)S(1)}, bf16[768,1024]{1,0:T(8,128)(2,1)S(1)}) fusion(f32[768,1024]{1,0:T(8,128)} %get-tuple-element.17, f32[768]{0:T(1024)S(1)} %fusion.40, f32[768,1024]{1,0:T(8,128)} %get-tuple-element.18, bf16[1,1024,3584]{2,1,0:T(8,128)(2,1)} %param.15, bf16[768,3712]{1,0:T(8,128)(2,1)} %reshape.155), kind=kOutput, calls=%fused_computation.27 | convolution fusion | flops 5641076736 | bytes 22285312 | tf_op jit(solution)/shard_map/dot_general | solution.py:8
  201.6 0.0 copy-start.5
  201.6 5.7 %fusion.14 = f32[768,1792]{1,0:T(8,128)S(1)} fusion(bf16[768,1024]{1,0:T(8,128)(2,1)S(1)} %get-tuple-element.29, bf16[1,3584,1024]{2,1,0:T(8,128)(2,1)} %param.14), kind=kOutput, calls=%fused_computation.18 | convolution fusion | flops 2818572288 | bytes 10747904 | tf_op jit(solution)/shard_map/dot_general | solution.py:8
  207.3 0.0 copy-done.5
  207.3 6.5 %add_convert_fusion.1 = bf16[768,1792]{1,0:T(8,128)(2,1)} fusion(f32[768,1792]{1,0:T(8,128)S(1)} %fusion.14, bf16[768,1024]{1,0:T(8,128)(2,1)S(1)} %get-tuple-element.28, bf16[1,3584,1024]{2,1,0:T(8,128)(2,1)} %param.13), kind=kOutput, calls=%fused_computation.12 | convolution fusion | flops 2821324800 | bytes 13500416 | tf_op jit(solution)/shard_map/dot_general | solution.py:8
  213.8 6.5 %reshape.158 = bf16[128,84,128]{2,1,0:T(8,128)(2,1)} reshape(bf16[768,1792]{1,0:T(8,128)(2,1)} %add_convert_fusion.1) | data formatting | bytes 5505024 | tf_op jit(solution)/shard_map/reshape | solution.py:49
  220.3 7.9 %all-to-all-start.2 = ((bf16[128,84,128]{2,1,0:T(8,128)(2,1)}), bf16[128,84,128]{2,1,0:T(8,128)(2,1)}, u32[]{:S(2)}, u32[]{:S(2)}) async-start(bf16[128,84,128]{2,1,0:T(8,128)(2,1)} %reshape.158), calls=%async_computation.2 | async-start | bytes 5767168 | tf_op jit(solution)/shard_map/all_to_all | solution.py:50
  228.2 0.0 slice-start.2
  228.2 7.0 %multiply_reduce_fusion = bf16[768]{0:T(1024)(128)(2,1)S(1)} fusion(f32[768,3584]{1,0:T(8,128)} %fusion.4, bf16[768,3712]{1,0:T(8,128)(2,1)} %reshape.155), kind=kLoop, calls=%fused_computation | loop fusion | flops 8256768 | bytes 16516608 | tf_op jit(solution)/shard_map/reduce_sum | solution.py:83
  235.2 0.7 convert_select_fusion
  235.8 0.2 reshape.163
  236.0 0.0 slice-start.3
  236.0 0.0 copy-start.6
  236.0 5.2 %fusion.10 = f32[768,1792]{1,0:T(8,128)S(1)} fusion(bf16[768,1024]{1,0:T(8,128)(2,1)S(1)} %get-tuple-element.29, bf16[1,3584,1024]{2,1,0:T(8,128)(2,1)} %param.14), kind=kOutput, calls=%fused_computation.14 | convolution fusion | flops 2818572288 | bytes 10747904 | tf_op jit(solution)/shard_map/dot_general | solution.py:8
  241.3 3.3 %add_convert_fusion = bf16[768,1792]{1,0:T(8,128)(2,1)S(1)} fusion(f32[768,1792]{1,0:T(8,128)S(1)} %fusion.10, bf16[768,1024]{1,0:T(8,128)(2,1)S(1)} %copy-done.6, bf16[1,3584,1024]{2,1,0:T(8,128)(2,1)S(1)} %bitcast.70), kind=kOutput, calls=%fused_computation.11 | convolution fusion | flops 2821324800 | bytes 13500416 | tf_op jit(solution)/shard_map/dot_general | solution.py:8
  244.6 1.8 fusion.27
  246.4 6.6 %reshape.161 = bf16[128,90,128]{2,1,0:T(8,128)(2,1)} reshape(bf16[768,1920]{1,0:T(8,128)(2,1)} %fusion.27) | data formatting | bytes 5898240 | tf_op jit(solution)/shard_map/reshape | solution.py:49
  253.1 13.3 %all-to-all-done.2 = bf16[128,84,128]{2,1,0:T(8,128)(2,1)} async-done(((bf16[128,84,128]{2,1,0:T(8,128)(2,1)}), bf16[128,84,128]{2,1,0:T(8,128)(2,1)}, u32[]{:S(2)}, u32[]{:S(2)}) %all-to-all-start.2) | async-done | bytes 2752544 | tf_op jit(solution)/shard_map/all_to_all | solution.py:50
  266.4 6.1 %all-to-all-start.3 = ((bf16[128,90,128]{2,1,0:T(8,128)(2,1)}), bf16[128,90,128]{2,1,0:T(8,128)(2,1)}, u32[]{:S(2)}, u32[]{:S(2)}) async-start(bf16[128,90,128]{2,1,0:T(8,128)(2,1)} %reshape.161), calls=%async_computation.3 | async-start | bytes 6291456 | tf_op jit(solution)/shard_map/all_to_all | solution.py:50
  272.5 6.2 %reshape.159 = bf16[768,1792]{1,0:T(8,128)(2,1)} reshape(bf16[128,84,128]{2,1,0:T(8,128)(2,1)} %all-to-all-done.2) | data formatting | bytes 5505024 | tf_op jit(solution)/shard_map/reshape | solution.py:51
  278.8 2.4 convolution_convert_fusion
  281.1 32.6 %all-to-all-done.3 = bf16[128,90,128]{2,1,0:T(8,128)(2,1)} async-done(((bf16[128,90,128]{2,1,0:T(8,128)(2,1)}), bf16[128,90,128]{2,1,0:T(8,128)(2,1)}, u32[]{:S(2)}, u32[]{:S(2)}) %all-to-all-start.3) | async-done | bytes 2949152 | tf_op jit(solution)/shard_map/all_to_all | solution.py:50
  313.8 6.5 %reshape.162 = bf16[768,1920]{1,0:T(8,128)(2,1)} reshape(bf16[128,90,128]{2,1,0:T(8,128)(2,1)} %all-to-all-done.3) | data formatting | bytes 5898240 | tf_op jit(solution)/shard_map/reshape | solution.py:51
  320.3 2.3 fusion.30
  322.7 1.4 fusion.34
  324.1 0.1 convert_element_type.60
  324.2 0.7 copy.34
  324.8 1.0 pad_maximum_fusion
  (22 shorter events, 0.1 us)
Async XLA Ops:
  0.6 3.0 copy-start
  18.7 12.0 %copy-start.4 = (bf16[128,4]{0,1:T(4,128)(2,1)S(1)}, bf16[128,4]{0,1:T(4,128)(2,1)}, u32[]{:S(2)}) copy-start(bf16[128,4]{0,1:T(4,128)(2,1)} %param.12) | copy-start | bytes 3076
  18.7 12.2 %copy-start.3 = (bf16[128,3584]{1,0:T(8,128)(2,1)S(1)}, bf16[128,3584]{1,0:T(8,128)(2,1)}, u32[]{:S(2)}) copy-start(bf16[128,3584]{1,0:T(8,128)(2,1)} %param.10) | copy-start | bytes 2752516
  18.7 80.4 %all-to-all-start.1 = ((bf16[128,168,128]{2,1,0:T(8,128)(2,1)}), bf16[128,168,128]{2,1,0:T(8,128)(2,1)}, u32[]{:S(2)}, u32[]{:S(2)}) async-start(bf16[128,168,128]{2,1,0:T(8,128)(2,1)} %reshape.156), calls=%async_computation.1 | async-start | bytes 11010048 | tf_op jit(solution)/shard_map/all_to_all | solution.py:50
  99.1 78.3 %all-to-all-start = ((bf16[128,174,128]{2,1,0:T(8,128)(2,1)}), bf16[128,174,128]{2,1,0:T(8,128)(2,1)}, u32[]{:S(2)}, u32[]{:S(2)}) async-start(bf16[128,174,128]{2,1,0:T(8,128)(2,1)} %reshape.154), calls=%async_computation | async-start | bytes 11534336 | tf_op jit(solution)/shard_map/all_to_all | solution.py:50
  118.2 9.9 %copy-start.2 = (bf16[768,3584]{1,0:T(8,128)(2,1)S(1)}, bf16[768,3584]{1,0:T(8,128)(2,1)}, u32[]{:S(2)}) copy-start(bf16[768,3584]{1,0:T(8,128)(2,1)} %reshape.157) | copy-start | bytes 16515076
  118.2 20.8 %slice-start = ((s8[7340032]{0:T(1024)(128)(4,1)}), s8[4194304]{0:T(1024)(128)(4,1)S(1)}, s32[]{:S(2)}) async-start(s8[7340032]{0:T(1024)(128)(4,1)} %bitcast.67), calls=%async_computation.4 | async-start | bytes 8388608
  128.0 10.9 %slice-start.1 = ((s8[7340032]{0:T(1024)(128)(4,1)}), s8[3145728]{0:T(1024)(128)(4,1)S(1)}, s32[]{:S(2)}) async-start(s8[7340032]{0:T(1024)(128)(4,1)} %bitcast.67), calls=%async_computation.5 | async-start | bytes 6291456
  201.6 5.7 %copy-start.5 = (bf16[768,1024]{1,0:T(8,128)(2,1)}, bf16[768,1024]{1,0:T(8,128)(2,1)S(1)}, u32[]{:S(2)}) copy-start(bf16[768,1024]{1,0:T(8,128)(2,1)S(1)} %get-tuple-element.28) | copy-start | bytes 4718596
  220.3 46.1 %all-to-all-start.2 = ((bf16[128,84,128]{2,1,0:T(8,128)(2,1)}), bf16[128,84,128]{2,1,0:T(8,128)(2,1)}, u32[]{:S(2)}, u32[]{:S(2)}) async-start(bf16[128,84,128]{2,1,0:T(8,128)(2,1)} %reshape.158), calls=%async_computation.2 | async-start | bytes 5767168 | tf_op jit(solution)/shard_map/all_to_all | solution.py:50
  228.2 13.1 %slice-start.2 = ((s8[7340032]{0:T(1024)(128)(4,1)}), s8[3145728]{0:T(1024)(128)(4,1)S(1)}, s32[]{:S(2)}) async-start(s8[7340032]{0:T(1024)(128)(4,1)} %bitcast.69), calls=%async_computation.6 | async-start | bytes 6291456
  236.0 5.3 %slice-start.3 = ((s8[7340032]{0:T(1024)(128)(4,1)}), s8[4194304]{0:T(1024)(128)(4,1)S(1)}, s32[]{:S(2)}) async-start(s8[7340032]{0:T(1024)(128)(4,1)} %bitcast.69), calls=%async_computation.7 | async-start | bytes 8388608
  236.0 5.3 %copy-start.6 = (bf16[768,1024]{1,0:T(8,128)(2,1)S(1)}, bf16[768,1024]{1,0:T(8,128)(2,1)}, u32[]{:S(2)}) copy-start(bf16[768,1024]{1,0:T(8,128)(2,1)} %copy-done.5) | copy-start | bytes 4718596
  266.4 47.4 %all-to-all-start.3 = ((bf16[128,90,128]{2,1,0:T(8,128)(2,1)}), bf16[128,90,128]{2,1,0:T(8,128)(2,1)}, u32[]{:S(2)}, u32[]{:S(2)}) async-start(bf16[128,90,128]{2,1,0:T(8,128)(2,1)} %reshape.161), calls=%async_computation.3 | async-start | bytes 6291456 | tf_op jit(solution)/shard_map/all_to_all | solution.py:50
  313.8 12.0 %copy-start.1 = (bf16[128,3584]{1,0:T(8,128)(2,1)S(1)}, bf16[128,3584]{1,0:T(8,128)(2,1)}, u32[]{:S(2)}) copy-start(bf16[128,3584]{1,0:T(8,128)(2,1)} %param.9) | copy-start | bytes 2752516
where the time goes:
time: 328 us; the launch traced here: 326 us
  waiting for transfers between devices  127 us (39%)
  matrix products  76.5 us (23%)
  local copies, waits for them, and re-layouts  73.5 us (22%)
  starting transfers between devices  33.7 us (10%)
  other arithmetic  14.1 us (4%)
    all_to_all x4, waiting for transfers between devices, a2a(): lax.all_to_all(v, ('group', 'local'), split_axis=0, concat_axis=0, tiled=...  127 us
    reshape x4, local copies, waits for them, and re-layouts, a2a(): v = v.reshape(expert_count, slot_cap * width // lane, lane)  36.1 us
    reshape x4, local copies, waits for them, and re-layouts, a2a(): return v.reshape(slot_total, width)  34.9 us
    all_to_all x4, starting transfers between devices, a2a(): lax.all_to_all(v, ('group', 'local'), split_axis=0, concat_axis=0, tiled=...  33.7 us
    dot_general x5, matrix products, _t_dot(): lax.dot_general(a, b, (((1,), (1,)), ((), ())), preferred_element_type=jn...  32.1 us
    dot_general x1, matrix products, local(): gate_pre = jnp.dot(rows_x, gate_mat, preferred_element_type=jnp.float32)  10.9 us
    dot_general x1, matrix products, local(): up_pre = jnp.dot(rows_x, up_mat, preferred_element_type=jnp.float32)  9.84 us
    dot_general x1, matrix products, local(): output = jnp.dot(hidden, down_mat, preferred_element_type=jnp.float32)  9.5 us
  transfers between devices with their start and end apart: 4, of which 4 were waited for; matrix products, arithmetic and copies ran while one was open for 28% of the time, Pallas kernels for 0%

commit v1 on v0

--- a/solution.py
+++ b/solution.py
@@ -1,6 +1,7 @@
 import jax
 import jax.numpy as jnp
 from jax import lax
+from jax.experimental.layout import Layout, with_layout_constraint
 from jax.sharding import PartitionSpec as P
 
 
@@ -50,15 +51,18 @@
         v = lax.all_to_all(v, ("group", "local"), split_axis=0, concat_axis=0, tiled=True)
         return v.reshape(slot_total, width)
 
+    row_major = Layout(major_to_minor=(0, 1))
+    gate_t, up_t, down_t = (
+        with_layout_constraint(w.T, row_major) for w in (gate_mat, up_mat, down_mat)
+    )
     rows_x = a2a(send_x)
     gate_pre = jnp.dot(rows_x, gate_mat, preferred_element_type=jnp.float32)
     up_pre = jnp.dot(rows_x, up_mat, preferred_element_type=jnp.float32)
     sigmoid_gate = jax.nn.sigmoid(gate_pre)
     active = gate_pre * sigmoid_gate
     hidden = (active * up_pre).astype(jnp.bfloat16)
-    output = jnp.dot(hidden, down_mat, preferred_element_type=jnp.float32)
     gate_factor = up_pre * sigmoid_gate * (1.0 + gate_pre * (1.0 - sigmoid_gate))
-    gate_factor, active, output = lax.optimization_barrier((gate_factor, active, output))
+    gate_factor, active, hidden = lax.optimization_barrier((gate_factor, active, hidden))
 
     rows_dyp = a2a(send_dyp)
     rows_dy = rows_dyp[:, :model_width]
@@ -67,20 +71,22 @@
     rows_p = jnp.sum(
         jnp.where(info_rows[:, top_count:] == e_me, info_rows[:, :top_count], 0.0), axis=1
     )
-    back_hidden = _t_dot(rows_dy, down_mat)
-    back_hidden = back_hidden * rows_p[:, None]
+    back_raw = jnp.dot(rows_dy, down_t, preferred_element_type=jnp.float32)
+    grad_weight = jnp.sum(hidden.astype(jnp.float32) * back_raw, axis=1).astype(jnp.bfloat16)
+    back_hidden = back_raw * rows_p[:, None]
     grad_gate = (back_hidden * gate_factor).astype(jnp.bfloat16)
     grad_up = (back_hidden * active).astype(jnp.bfloat16)
 
     half = model_width // 2
-    contrib_a = (_t_dot(grad_gate, gate_mat[:half]) + _t_dot(grad_up, up_mat[:half])).astype(
-        jnp.bfloat16
-    )
+    contrib_a = (
+        jnp.dot(grad_gate, gate_t[:, :half], preferred_element_type=jnp.float32)
+        + jnp.dot(grad_up, up_t[:, :half], preferred_element_type=jnp.float32)
+    ).astype(jnp.bfloat16)
     back_a = a2a(contrib_a)
-    contrib_b = (_t_dot(grad_gate, gate_mat[half:]) + _t_dot(grad_up, up_mat[half:])).astype(
-        jnp.bfloat16
-    )
-    grad_weight = jnp.sum(rows_dy.astype(jnp.float32) * output, axis=1).astype(jnp.bfloat16)
+    contrib_b = (
+        jnp.dot(grad_gate, gate_t[:, half:], preferred_element_type=jnp.float32)
+        + jnp.dot(grad_up, up_t[:, half:], preferred_element_type=jnp.float32)
+    ).astype(jnp.bfloat16)
     gw_block = jnp.zeros((slot_total, lane), jnp.bfloat16).at[:, 0].set(grad_weight)
     back_b = a2a(jnp.concatenate([contrib_b, gw_block], axis=1))
 

time: 328 us -> 329 us (level)
  local copies, waits for them, and re-layouts: 73.5 us -> 104 us
  waiting for transfers between devices: 127 us -> 109 us
  other arithmetic: 14.1 us -> 7.13 us
  matrix products: 76.5 us -> 71.5 us
    unnamed x24 -> x19, local copies, waits for them, and re-layouts: 1.59 us -> 32.1 us
    all_to_all x4, waiting for transfers between devices: 127 us -> 109 us  [a2a(): lax.all_to_all(v, ('group', 'local'), split_axis=0, concat_axis=0, tiled=...]
    reduce_sum x1 -> x0, other arithmetic: 6.99 us -> none  [local(): jnp.sum(rows_dy.astype(jnp.float32) * output, axis=1).astype(jnp.bfloat16)]
    dot_general x6 -> x5, matrix products: 41.6 us -> 34.8 us  [the longest x1 12.1 us: local(): back_raw = jnp.dot(rows_dy, down_t, preferred_element_type=jnp.float32)]
  transfers between devices with their start and end apart: 4 -> 4, of which waited for: 4 -> 4; matrix products, arithmetic and copies ran while one was open for 28% -> 33% of each run, Pallas kernels for 0% -> 0%
where the time goes in v1:
time: 329 us; the launch traced here: 326 us
  waiting for transfers between devices  109 us (33%)
  local copies, waits for them, and re-layouts  104 us (32%)
  matrix products  71.5 us (22%)
  starting transfers between devices  33.4 us (10%)
  other arithmetic  7.13 us (2%)
    all_to_all x4, waiting for transfers between devices, a2a(): lax.all_to_all(v, ('group', 'local'), split_axis=0, concat_axis=0, tiled=...  109 us
    reshape x4, local copies, waits for them, and re-layouts, a2a(): v = v.reshape(expert_count, slot_cap * width // lane, lane)  36.1 us
    reshape x4, local copies, waits for them, and re-layouts, a2a(): return v.reshape(slot_total, width)  34.9 us
    all_to_all x4, starting transfers between devices, a2a(): lax.all_to_all(v, ('group', 'local'), split_axis=0, concat_axis=0, tiled=...  33.4 us
    unnamed x19, local copies, waits for them, and re-layouts  32.1 us
    dot_general x1, matrix products, local(): back_raw = jnp.dot(rows_dy, down_t, preferred_element_type=jnp.float32)  12.1 us
    dot_general x1, matrix products, local(): up_pre = jnp.dot(rows_x, up_mat, preferred_element_type=jnp.float32)  12 us
    dot_general x1, matrix products, local(): gate_pre = jnp.dot(rows_x, gate_mat, preferred_element_type=jnp.float32)  10.5 us
  transfers between devices with their start and end apart: 4, of which 4 were waited for; matrix products, arithmetic and copies ran while one was open for 33% of the time, Pallas kernels for 0%

profile of v1, /device:TPU:1, one launch (start us, length us, event | category | flops | bytes accessed | tf_op | source)
XLA Modules:
  0.0 326.3 jit_solution(5469786725935667671)
XLA Ops:
  0.6 0.0 copy-start
  0.6 0.9 copy.37
  1.5 0.1 eq.143
  1.6 0.1 eq.139
  1.7 0.1 copy.39
  1.8 0.2 fusion.36
  2.1 0.1 add_add_fusion
  2.2 0.2 fusion.35
  2.4 0.1 reduce_sum.30
  2.5 0.1 copy.41
  2.6 0.8 fusion.42
  3.4 0.2 fusion.27
  3.6 0.0 copy-done
  3.6 4.0 %fusion.43 = bf16[768,3584]{1,0:T(8,128)(2,1)} fusion(pred[768,128]{1,0:T(8,128)(4,1)S(1)} %fusion.27, bf16[128,3584]{1,0:T(8,128)(2,1)S(1)} %copy-done), kind=kOutput, calls=%fused_computation.80 | convolution fusion | flops 704643072 | bytes 6520832 | tf_op jit(solution)/shard_map/dot_general | solution.py:38
  7.6 11.1 %reshape.152 = bf16[128,168,128]{2,1,0:T(8,128)(2,1)} reshape(bf16[768,3584]{1,0:T(8,128)(2,1)} %fusion.43) | data formatting | bytes 11010048 | tf_op jit(solution)/shard_map/reshape | solution.py:50
  18.7 0.0 copy-start.4
  18.7 0.0 copy-start.3
  18.7 11.9 %all-to-all-start.1 = ((bf16[128,168,128]{2,1,0:T(8,128)(2,1)}), bf16[128,168,128]{2,1,0:T(8,128)(2,1)}, u32[]{:S(2)}, u32[]{:S(2)}) async-start(bf16[128,168,128]{2,1,0:T(8,128)(2,1)} %reshape.152), calls=%async_computation.1 | async-start | bytes 11010048 | tf_op jit(solution)/shard_map/all_to_all | solution.py:51
  30.7 0.0 copy-done.4
  30.7 0.2 select_select_fusion
  30.9 0.0 copy-done.3
  30.9 4.1 %fusion.29 = bf16[768,3712]{1,0:T(8,128)(2,1)} fusion(pred[768,128]{1,0:T(8,128)(4,1)S(1)} %fusion.27, bf16[128,128]{1,0:T(8,128)(2,1)S(1)} %select_select_fusion, bf16[128,3584]{1,0:T(8,128)(2,1)S(1)} %copy-done.3), kind=kOutput, calls=%fused_computation.35 | convolution fusion | flops 731709440 | bytes 6750208 | tf_op jit(solution)/shard_map/dot_general | solution.py:44
  35.0 11.9 %reshape.150 = bf16[128,174,128]{2,1,0:T(8,128)(2,1)} reshape(bf16[768,3712]{1,0:T(8,128)(2,1)} %fusion.29) | data formatting | bytes 11403264 | tf_op jit(solution)/shard_map/reshape | solution.py:50
  46.9 52.2 %all-to-all-done.1 = bf16[128,168,128]{2,1,0:T(8,128)(2,1)} async-done(((bf16[128,168,128]{2,1,0:T(8,128)(2,1)}), bf16[128,168,128]{2,1,0:T(8,128)(2,1)}, u32[]{:S(2)}, u32[]{:S(2)}) %all-to-all-start.1) | async-done | bytes 5505056 | tf_op jit(solution)/shard_map/all_to_all | solution.py:51
  99.1 7.8 %all-to-all-start = ((bf16[128,174,128]{2,1,0:T(8,128)(2,1)}), bf16[128,174,128]{2,1,0:T(8,128)(2,1)}, u32[]{:S(2)}, u32[]{:S(2)}) async-start(bf16[128,174,128]{2,1,0:T(8,128)(2,1)} %reshape.150), calls=%async_computation | async-start | bytes 11534336 | tf_op jit(solution)/shard_map/all_to_all | solution.py:51
  106.9 10.4 %copy.42 = bf16[1,1024,3584]{1,2,0:T(8,128)(2,1)} copy(bf16[1,1024,3584]{2,1,0:T(8,128)(2,1)} %param.15) | data formatting | bytes 14680064 | tf_op args[6]
  117.3 10.1 %copy.43 = bf16[1,3584,1024]{1,2,0:T(8,128)(2,1)} copy(bf16[1,3584,1024]{2,1,0:T(8,128)(2,1)} %param.14) | data formatting | bytes 14680064 | tf_op args[5]
  127.4 10.0 %copy.44 = bf16[1,3584,1024]{1,2,0:T(8,128)(2,1)} copy(bf16[1,3584,1024]{2,1,0:T(8,128)(2,1)} %param.13) | data formatting | bytes 14680064 | tf_op args[4]
  137.4 10.6 %reshape.153 = bf16[768,3584]{1,0:T(8,128)(2,1)} reshape(bf16[128,168,128]{2,1,0:T(8,128)(2,1)} %all-to-all-done.1) | data formatting | bytes 11010048 | tf_op jit(solution)/shard_map/reshape | solution.py:52
  148.1 10.5 %fusion = f32[768,1024]{1,0:T(8,128)S(1)} fusion(bf16[768,3584]{1,0:T(8,128)(2,1)} %reshape.153, bf16[1,3584,1024]{2,1,0:T(8,128)(2,1)} %param.13), kind=kOutput, calls=%fused_computation | convolution fusion | flops 5637144576 | bytes 15990784 | tf_op jit(solution)/shard_map/dot_general | solution.py:59
  158.6 0.0 copy-done.2
  158.6 12.0 %multiply_convert_fusion.2 = (bf16[768,1024]{1,0:T(8,128)(2,1)}, f32[768,1024]{1,0:T(8,128)}, f32[768,1024]{1,0:T(8,128)}) fusion(f32[768,1024]{1,0:T(8,128)S(1)} %fusion, bf16[768,3584]{1,0:T(8,128)(2,1)S(1)} %copy-done.2, bf16[1,3584,1024]{2,1,0:T(8,128)(2,1)} %param.14), kind=kOutput, calls=%fused_computation.22 | convolution fusion | flops 5645795328 | bytes 23855104 | tf_op jit(solution)/shard_map/dot_general | solution.py:60
  170.7 6.8 %all-to-all-done = bf16[128,174,128]{2,1,0:T(8,128)(2,1)} async-done(((bf16[128,174,128]{2,1,0:T(8,128)(2,1)}), bf16[128,174,128]{2,1,0:T(8,128)(2,1)}, u32[]{:S(2)}, u32[]{:S(2)}) %all-to-all-start) | async-done | bytes 5701664 | tf_op jit(solution)/shard_map/all_to_all | solution.py:51
  177.4 11.5 %reshape.151 = bf16[768,3712]{1,0:T(8,128)(2,1)} reshape(bf16[128,174,128]{2,1,0:T(8,128)(2,1)} %all-to-all-done) | data formatting | bytes 11403264 | tf_op jit(solution)/shard_map/reshape | solution.py:52
  189.0 1.0 slice_convert_fusion
  189.9 0.3 fusion.34
  190.2 12.1 %multiply_convert_fusion.1 = (bf16[768,1024]{1,0:T(8,128)(2,1)S(1)}, bf16[768,1024]{1,0:T(8,128)(2,1)S(1)}, bf16[768]{0:T(1024)(128)(2,1)S(1)}) fusion(f32[768,1024]{1,0:T(8,128)} %get-tuple-element.17, f32[768]{0:T(1024)S(1)} %fusion.34, f32[768,1024]{1,0:T(8,128)} %get-tuple-element.18, bf16[768,1024]{1,0:T(8,128)(2,1)} %get-tuple-element.19, ...), kind=kOutput, calls=%fused_computation.21 | convolution fusion | flops 5643435008 | bytes 23859712 | tf_op jit(solution)/shard_map/dot_general | solution.py:74
  202.3 0.0 copy-start.5
  202.3 5.6 %fusion.12 = f32[768,1792]{1,0:T(8,128)S(1)} fusion(bf16[768,1024]{1,0:T(8,128)(2,1)S(1)} %get-tuple-element.31, bf16[1024,3584]{1,0:T(8,128)(2,1)} %bitcast.59), kind=kOutput, calls=%fused_computation.15 | convolution fusion | flops 2818572288 | bytes 10747904 | tf_op jit(solution)/shard_map/dot_general | solution.py:83
  208.0 0.0 copy-done.5
  208.0 6.6 %add_convert_fusion.1 = bf16[768,1792]{1,0:T(8,128)(2,1)} fusion(f32[768,1792]{1,0:T(8,128)S(1)} %fusion.12, bf16[768,1024]{1,0:T(8,128)(2,1)S(1)} %get-tuple-element.30, bf16[1024,3584]{1,0:T(8,128)(2,1)} %bitcast.57), kind=kOutput, calls=%fused_computation.10 | convolution fusion | flops 2821324800 | bytes 13500416 | tf_op jit(solution)/shard_map/dot_general | solution.py:82
  214.6 6.4 %reshape.154 = bf16[128,84,128]{2,1,0:T(8,128)(2,1)} reshape(bf16[768,1792]{1,0:T(8,128)(2,1)} %add_convert_fusion.1) | data formatting | bytes 5505024 | tf_op jit(solution)/shard_map/reshape | solution.py:50
  221.0 7.9 %all-to-all-start.2 = ((bf16[128,84,128]{2,1,0:T(8,128)(2,1)}), bf16[128,84,128]{2,1,0:T(8,128)(2,1)}, u32[]{:S(2)}, u32[]{:S(2)}) async-start(bf16[128,84,128]{2,1,0:T(8,128)(2,1)} %reshape.154), calls=%async_computation.2 | async-start | bytes 5767168 | tf_op jit(solution)/shard_map/all_to_all | solution.py:51
  228.9 0.6 compare_reduce_fusion
  229.6 0.6 convert_select_fusion
  230.2 0.2 reshape.159
  230.4 0.0 copy-start.6
  230.4 5.2 %fusion.8 = f32[768,1792]{1,0:T(8,128)S(1)} fusion(bf16[768,1024]{1,0:T(8,128)(2,1)S(1)} %get-tuple-element.31, bf16[1024,3584]{1,0:T(8,128)(2,1)} %bitcast.60), kind=kOutput, calls=%fused_computation.11 | convolution fusion | flops 2818572288 | bytes 10747904 | tf_op jit(solution)/shard_map/dot_general | solution.py:88
  235.6 0.0 copy-done.6
  235.6 5.3 %add_convert_fusion = bf16[768,1792]{1,0:T(8,128)(2,1)S(1)} fusion(f32[768,1792]{1,0:T(8,128)S(1)} %fusion.8, bf16[768,1024]{1,0:T(8,128)(2,1)S(1)} %copy-done.6, bf16[1024,3584]{1,0:T(8,128)(2,1)} %bitcast.58), kind=kOutput, calls=%fused_computation.9 | convolution fusion | flops 2821324800 | bytes 13500416 | tf_op jit(solution)/shard_map/dot_general | solution.py:87
  240.9 1.8 fusion.21
  242.8 6.6 %reshape.157 = bf16[128,90,128]{2,1,0:T(8,128)(2,1)} reshape(bf16[768,1920]{1,0:T(8,128)(2,1)} %fusion.21) | data formatting | bytes 5898240 | tf_op jit(solution)/shard_map/reshape | solution.py:50
  249.4 17.8 %all-to-all-done.2 = bf16[128,84,128]{2,1,0:T(8,128)(2,1)} async-done(((bf16[128,84,128]{2,1,0:T(8,128)(2,1)}), bf16[128,84,128]{2,1,0:T(8,128)(2,1)}, u32[]{:S(2)}, u32[]{:S(2)}) %all-to-all-start.2) | async-done | bytes 2752544 | tf_op jit(solution)/shard_map/all_to_all | solution.py:51
  267.1 5.9 %all-to-all-start.3 = ((bf16[128,90,128]{2,1,0:T(8,128)(2,1)}), bf16[128,90,128]{2,1,0:T(8,128)(2,1)}, u32[]{:S(2)}, u32[]{:S(2)}) async-start(bf16[128,90,128]{2,1,0:T(8,128)(2,1)} %reshape.157), calls=%async_computation.3 | async-start | bytes 6291456 | tf_op jit(solution)/shard_map/all_to_all | solution.py:51
  273.0 6.3 %reshape.155 = bf16[768,1792]{1,0:T(8,128)(2,1)} reshape(bf16[128,84,128]{2,1,0:T(8,128)(2,1)} %all-to-all-done.2) | data formatting | bytes 5505024 | tf_op jit(solution)/shard_map/reshape | solution.py:52
  279.3 2.4 convolution_convert_fusion
  281.6 32.6 %all-to-all-done.3 = bf16[128,90,128]{2,1,0:T(8,128)(2,1)} async-done(((bf16[128,90,128]{2,1,0:T(8,128)(2,1)}), bf16[128,90,128]{2,1,0:T(8,128)(2,1)}, u32[]{:S(2)}, u32[]{:S(2)}) %all-to-all-start.3) | async-done | bytes 2949152 | tf_op jit(solution)/shard_map/all_to_all | solution.py:51
  314.3 6.5 %reshape.158 = bf16[768,1920]{1,0:T(8,128)(2,1)} reshape(bf16[128,90,128]{2,1,0:T(8,128)(2,1)} %all-to-all-done.3) | data formatting | bytes 5898240 | tf_op jit(solution)/shard_map/reshape | solution.py:52
  320.8 2.4 fusion.24
  323.2 1.4 fusion.28
  324.5 0.1 convert_element_type.60
  324.7 0.7 copy.46
  325.3 1.0 pad_maximum_fusion
  326.3 0.0 copy-done.1
  (13 shorter events, 0.1 us)
Async XLA Ops:
  0.6 3.0 copy-start
  18.7 12.0 %copy-start.4 = (bf16[128,4]{0,1:T(4,128)(2,1)S(1)}, bf16[128,4]{0,1:T(4,128)(2,1)}, u32[]{:S(2)}) copy-start(bf16[128,4]{0,1:T(4,128)(2,1)} %param.12) | copy-start | bytes 3076
  18.7 12.2 %copy-start.3 = (bf16[128,3584]{1,0:T(8,128)(2,1)S(1)}, bf16[128,3584]{1,0:T(8,128)(2,1)}, u32[]{:S(2)}) copy-start(bf16[128,3584]{1,0:T(8,128)(2,1)} %param.10) | copy-start | bytes 2752516
  18.7 80.4 %all-to-all-start.1 = ((bf16[128,168,128]{2,1,0:T(8,128)(2,1)}), bf16[128,168,128]{2,1,0:T(8,128)(2,1)}, u32[]{:S(2)}, u32[]{:S(2)}) async-start(bf16[128,168,128]{2,1,0:T(8,128)(2,1)} %reshape.152), calls=%async_computation.1 | async-start | bytes 11010048 | tf_op jit(solution)/shard_map/all_to_all | solution.py:51
  99.1 78.3 %all-to-all-start = ((bf16[128,174,128]{2,1,0:T(8,128)(2,1)}), bf16[128,174,128]{2,1,0:T(8,128)(2,1)}, u32[]{:S(2)}, u32[]{:S(2)}) async-start(bf16[128,174,128]{2,1,0:T(8,128)(2,1)} %reshape.150), calls=%async_computation | async-start | bytes 11534336 | tf_op jit(solution)/shard_map/all_to_all | solution.py:51
  148.1 10.5 %copy-start.2 = (bf16[768,3584]{1,0:T(8,128)(2,1)S(1)}, bf16[768,3584]{1,0:T(8,128)(2,1)}, u32[]{:S(2)}) copy-start(bf16[768,3584]{1,0:T(8,128)(2,1)} %reshape.153) | copy-start | bytes 16515076
  202.3 5.6 %copy-start.5 = (bf16[768,1024]{1,0:T(8,128)(2,1)}, bf16[768,1024]{1,0:T(8,128)(2,1)S(1)}, u32[]{:S(2)}) copy-start(bf16[768,1024]{1,0:T(8,128)(2,1)S(1)} %get-tuple-element.30) | copy-start | bytes 4718596
  221.0 46.1 %all-to-all-start.2 = ((bf16[128,84,128]{2,1,0:T(8,128)(2,1)}), bf16[128,84,128]{2,1,0:T(8,128)(2,1)}, u32[]{:S(2)}, u32[]{:S(2)}) async-start(bf16[128,84,128]{2,1,0:T(8,128)(2,1)} %reshape.154), calls=%async_computation.2 | async-start | bytes 5767168 | tf_op jit(solution)/shard_map/all_to_all | solution.py:51
  230.4 5.2 %copy-start.6 = (bf16[768,1024]{1,0:T(8,128)(2,1)S(1)}, bf16[768,1024]{1,0:T(8,128)(2,1)}, u32[]{:S(2)}) copy-start(bf16[768,1024]{1,0:T(8,128)(2,1)} %copy-done.5) | copy-start | bytes 4718596
  267.1 47.1 %all-to-all-start.3 = ((bf16[128,90,128]{2,1,0:T(8,128)(2,1)}), bf16[128,90,128]{2,1,0:T(8,128)(2,1)}, u32[]{:S(2)}, u32[]{:S(2)}) async-start(bf16[128,90,128]{2,1,0:T(8,128)(2,1)} %reshape.157), calls=%async_computation.3 | async-start | bytes 6291456 | tf_op jit(solution)/shard_map/all_to_all | solution.py:51
  314.3 12.0 %copy-start.1 = (bf16[128,3584]{1,0:T(8,128)(2,1)S(1)}, bf16[128,3584]{1,0:T(8,128)(2,1)}, u32[]{:S(2)}) copy-start(bf16[128,3584]{1,0:T(8,128)(2,1)} %param.9) | copy-start | bytes 2752516

commit v2 on v0

--- a/solution.py
+++ b/solution.py
@@ -56,9 +56,8 @@
     sigmoid_gate = jax.nn.sigmoid(gate_pre)
     active = gate_pre * sigmoid_gate
     hidden = (active * up_pre).astype(jnp.bfloat16)
-    output = jnp.dot(hidden, down_mat, preferred_element_type=jnp.float32)
     gate_factor = up_pre * sigmoid_gate * (1.0 + gate_pre * (1.0 - sigmoid_gate))
-    gate_factor, active, output = lax.optimization_barrier((gate_factor, active, output))
+    gate_factor, active, hidden = lax.optimization_barrier((gate_factor, active, hidden))
 
     rows_dyp = a2a(send_dyp)
     rows_dy = rows_dyp[:, :model_width]
@@ -67,27 +66,27 @@
     rows_p = jnp.sum(
         jnp.where(info_rows[:, top_count:] == e_me, info_rows[:, :top_count], 0.0), axis=1
     )
-    back_hidden = _t_dot(rows_dy, down_mat)
-    back_hidden = back_hidden * rows_p[:, None]
+    back_raw = _t_dot(rows_dy, down_mat)
+    grad_weight = jnp.sum(hidden.astype(jnp.float32) * back_raw, axis=1).astype(jnp.bfloat16)
+    back_hidden = back_raw * rows_p[:, None]
     grad_gate = (back_hidden * gate_factor).astype(jnp.bfloat16)
     grad_up = (back_hidden * active).astype(jnp.bfloat16)
 
-    half = model_width // 2
+    half = model_width * 3 // 7 // (lane // 2) * (lane // 2)
     contrib_a = (_t_dot(grad_gate, gate_mat[:half]) + _t_dot(grad_up, up_mat[:half])).astype(
         jnp.bfloat16
     )
-    back_a = a2a(contrib_a)
+    gw_block = jnp.zeros((slot_total, lane), jnp.bfloat16).at[:, 0].set(grad_weight)
+    back_a = a2a(jnp.concatenate([contrib_a, gw_block], axis=1))
     contrib_b = (_t_dot(grad_gate, gate_mat[half:]) + _t_dot(grad_up, up_mat[half:])).astype(
         jnp.bfloat16
     )
-    grad_weight = jnp.sum(rows_dy.astype(jnp.float32) * output, axis=1).astype(jnp.bfloat16)
-    gw_block = jnp.zeros((slot_total, lane), jnp.bfloat16).at[:, 0].set(grad_weight)
-    back_b = a2a(jnp.concatenate([contrib_b, gw_block], axis=1))
+    back_b = a2a(contrib_b)
 
-    sum_a = jnp.dot(sel_t.T, back_a, preferred_element_type=jnp.float32)
-    sum_b = jnp.dot(sel_t.T, back_b[:, : model_width - half], preferred_element_type=jnp.float32)
+    sum_a = jnp.dot(sel_t.T, back_a[:, :half], preferred_element_type=jnp.float32)
+    sum_b = jnp.dot(sel_t.T, back_b, preferred_element_type=jnp.float32)
     grad_tokens = jnp.concatenate([sum_a, sum_b], axis=1).astype(jnp.bfloat16)
-    gw_back = jnp.dot(sel_a.T, back_b[:, model_width - half :], preferred_element_type=jnp.float32)
+    gw_back = jnp.dot(sel_a.T, back_a[:, half:], preferred_element_type=jnp.float32)
     grad_combine = gw_back[:, 0].astype(jnp.bfloat16).reshape(token_rows, top_count)
     return (grad_tokens, grad_combine)
 

time: 328 us -> 319 us (0.973)
  waiting for transfers between devices: 127 us -> 140 us
  other arithmetic: 14.1 us -> 5.48 us
  matrix products: 76.5 us -> 70.6 us
  local copies, waits for them, and re-layouts: 73.5 us -> 67.6 us
    all_to_all x4, waiting for transfers between devices: 127 us -> 140 us  [a2a(): lax.all_to_all(v, ('group', 'local'), split_axis=0, concat_axis=0, tiled=...]
    dot_general x4 -> x3, matrix products: 15.5 us -> 6.05 us  [the longest x1 2.51 us: local(): sum_b = jnp.dot(sel_t.T, back_b, preferred_element_type=jnp.float32)]
    reduce_sum x1 -> x0, other arithmetic: 6.99 us -> none  [local(): jnp.sum(rows_dy.astype(jnp.float32) * output, axis=1).astype(jnp.bfloat16)]
  transfers between devices with their start and end apart: 4 -> 4, of which waited for: 4 -> 4; matrix products, arithmetic and copies ran while one was open for 28% -> 24% of each run, Pallas kernels for 0% -> 0%
where the time goes in v2:
time: 319 us; the launch traced here: 317 us
  waiting for transfers between devices  140 us (44%)
  matrix products  70.6 us (22%)
  local copies, waits for them, and re-layouts  67.6 us (21%)
  starting transfers between devices  32.9 us (10%)
  other arithmetic  5.48 us (2%)
    all_to_all x4, waiting for transfers between devices, a2a(): lax.all_to_all(v, ('group', 'local'), split_axis=0, concat_axis=0, tiled=...  140 us
    dot_general x5, matrix products, _t_dot(): lax.dot_general(a, b, (((1,), (1,)), ((), ())), preferred_element_type=jn...  35.1 us
    reshape x4, local copies, waits for them, and re-layouts, a2a(): v = v.reshape(expert_count, slot_cap * width // lane, lane)  33.1 us
    all_to_all x4, starting transfers between devices, a2a(): lax.all_to_all(v, ('group', 'local'), split_axis=0, concat_axis=0, tiled=...  32.9 us
    reshape x4, local copies, waits for them, and re-layouts, a2a(): return v.reshape(slot_total, width)  32 us
    dot_general x1, matrix products, local(): up_pre = jnp.dot(rows_x, up_mat, preferred_element_type=jnp.float32)  10.7 us
    dot_general x1, matrix products, local(): gate_pre = jnp.dot(rows_x, gate_mat, preferred_element_type=jnp.float32)  10.6 us
  transfers between devices with their start and end apart: 4, of which 4 were waited for; matrix products, arithmetic and copies ran while one was open for 24% of the time, Pallas kernels for 0%

profile of v2, /device:TPU:1, one launch (start us, length us, event | category | flops | bytes accessed | tf_op | source)
XLA Modules:
  0.0 317.4 jit_solution(8870485851046680352)
XLA Ops:
  0.6 0.0 copy-start
  0.6 0.9 copy.28
  1.5 0.1 eq.143
  1.6 0.1 eq.139
  1.7 0.1 copy.30
  1.8 0.2 fusion.33
  2.1 0.1 add_add_fusion
  2.2 0.2 fusion.32
  2.4 0.1 reduce_sum.30
  2.5 0.1 copy.32
  2.6 0.8 fusion.39
  3.4 0.2 fusion.24
  3.6 0.0 copy-done
  3.6 0.0 copy-start.3
  3.6 4.0 %fusion.40 = bf16[768,3584]{1,0:T(8,128)(2,1)} fusion(pred[768,128]{1,0:T(8,128)(4,1)S(1)} %fusion.24, bf16[128,3584]{1,0:T(8,128)(2,1)S(1)} %copy-done), kind=kOutput, calls=%fused_computation.82 | convolution fusion | flops 704643072 | bytes 6520832 | tf_op jit(solution)/shard_map/dot_general | solution.py:37
  7.6 11.2 %reshape.156 = bf16[128,168,128]{2,1,0:T(8,128)(2,1)} reshape(bf16[768,3584]{1,0:T(8,128)(2,1)} %fusion.40) | data formatting | bytes 11010048 | tf_op jit(solution)/shard_map/reshape | solution.py:49
  18.7 11.9 %all-to-all-start.1 = ((bf16[128,168,128]{2,1,0:T(8,128)(2,1)}), bf16[128,168,128]{2,1,0:T(8,128)(2,1)}, u32[]{:S(2)}, u32[]{:S(2)}) async-start(bf16[128,168,128]{2,1,0:T(8,128)(2,1)} %reshape.156), calls=%async_computation.1 | async-start | bytes 11010048 | tf_op jit(solution)/shard_map/all_to_all | solution.py:50
  30.7 0.0 copy-done.7
  30.7 0.2 select_select_fusion
  30.9 0.0 copy-done.3
  30.9 0.0 copy-done.6
  31.0 4.2 %fusion.26 = bf16[768,3712]{1,0:T(8,128)(2,1)} fusion(pred[768,128]{1,0:T(8,128)(4,1)S(1)} %fusion.24, bf16[128,128]{1,0:T(8,128)(2,1)S(1)} %select_select_fusion, bf16[128,3584]{1,0:T(8,128)(2,1)S(1)} %copy-done.6), kind=kOutput, calls=%fused_computation.37 | convolution fusion | flops 731709440 | bytes 6750208 | tf_op jit(solution)/shard_map/dot_general | solution.py:43
  35.1 11.9 %reshape.154 = bf16[128,174,128]{2,1,0:T(8,128)(2,1)} reshape(bf16[768,3712]{1,0:T(8,128)(2,1)} %fusion.26) | data formatting | bytes 11403264 | tf_op jit(solution)/shard_map/reshape | solution.py:49
  47.1 52.1 %all-to-all-done.1 = bf16[128,168,128]{2,1,0:T(8,128)(2,1)} async-done(((bf16[128,168,128]{2,1,0:T(8,128)(2,1)}), bf16[128,168,128]{2,1,0:T(8,128)(2,1)}, u32[]{:S(2)}, u32[]{:S(2)}) %all-to-all-start.1) | async-done | bytes 5505056 | tf_op jit(solution)/shard_map/all_to_all | solution.py:50
  99.2 7.8 %all-to-all-start = ((bf16[128,174,128]{2,1,0:T(8,128)(2,1)}), bf16[128,174,128]{2,1,0:T(8,128)(2,1)}, u32[]{:S(2)}, u32[]{:S(2)}) async-start(bf16[128,174,128]{2,1,0:T(8,128)(2,1)} %reshape.154), calls=%async_computation | async-start | bytes 11534336 | tf_op jit(solution)/shard_map/all_to_all | solution.py:50
  106.9 0.6 compare_reduce_fusion
  107.6 10.7 %reshape.157 = bf16[768,3584]{1,0:T(8,128)(2,1)} reshape(bf16[128,168,128]{2,1,0:T(8,128)(2,1)} %all-to-all-done.1) | data formatting | bytes 11010048 | tf_op jit(solution)/shard_map/reshape | solution.py:51
  118.2 10.6 %fusion = f32[768,1024]{1,0:T(8,128)S(1)} fusion(bf16[768,3584]{1,0:T(8,128)(2,1)} %reshape.157, bf16[1,3584,1024]{2,1,0:T(8,128)(2,1)} %param.13), kind=kOutput, calls=%fused_computation | convolution fusion | flops 5637144576 | bytes 15990784 | tf_op jit(solution)/shard_map/dot_general | solution.py:54
  128.8 0.0 copy-done.2
  128.8 10.7 %multiply_convert_fusion.2 = (bf16[768,1024]{1,0:T(8,128)(2,1)S(1)}, f32[768,1024]{1,0:T(8,128)}, f32[768,1024]{1,0:T(8,128)}) fusion(f32[768,1024]{1,0:T(8,128)S(1)} %fusion, bf16[768,3584]{1,0:T(8,128)(2,1)S(1)} %copy-done.2, bf16[1,3584,1024]{2,1,0:T(8,128)(2,1)} %param.14), kind=kOutput, calls=%fused_computation.25 | convolution fusion | flops 5645795328 | bytes 23855104 | tf_op jit(solution)/shard_map/dot_general | solution.py:55
  139.6 37.9 %all-to-all-done = bf16[128,174,128]{2,1,0:T(8,128)(2,1)} async-done(((bf16[128,174,128]{2,1,0:T(8,128)(2,1)}), bf16[128,174,128]{2,1,0:T(8,128)(2,1)}, u32[]{:S(2)}, u32[]{:S(2)}) %all-to-all-start) | async-done | bytes 5701664 | tf_op jit(solution)/shard_map/all_to_all | solution.py:50
  177.5 11.5 %reshape.155 = bf16[768,3712]{1,0:T(8,128)(2,1)} reshape(bf16[128,174,128]{2,1,0:T(8,128)(2,1)} %all-to-all-done) | data formatting | bytes 11403264 | tf_op jit(solution)/shard_map/reshape | solution.py:51
  189.0 1.0 slice_convert_fusion
  189.9 0.3 fusion.31
  190.2 11.6 %multiply_convert_fusion.1 = (bf16[768,1024]{1,0:T(8,128)(2,1)S(1)}, bf16[768,1024]{1,0:T(8,128)(2,1)S(1)}, bf16[768]{0:T(1024)(128)(2,1)S(1)}) fusion(f32[768,1024]{1,0:T(8,128)} %get-tuple-element.17, f32[768]{0:T(1024)S(1)} %fusion.31, f32[768,1024]{1,0:T(8,128)} %get-tuple-element.18, bf16[768,1024]{1,0:T(8,128)(2,1)S(1)} %get-tuple-element.19, ...), kind=kOutput, calls=%fused_computation.24 | convolution fusion | flops 5643435008 | bytes 23859712 | tf_op jit(solution)/shard_map/dot_general | solution.py:8
  201.9 0.0 copy-start.8
  201.9 5.7 %fusion.15 = f32[768,1536]{1,0:T(8,128)S(1)} fusion(bf16[768,1024]{1,0:T(8,128)(2,1)S(1)} %get-tuple-element.30, bf16[1,3584,1024]{2,1,0:T(8,128)(2,1)} %param.13), kind=kOutput, calls=%fused_computation.18 | convolution fusion | flops 2415919104 | bytes 9437184 | tf_op jit(solution)/shard_map/dot_general | solution.py:8
  207.6 0.0 copy-done.8
  207.6 0.7 convert_select_fusion
  208.3 0.2 reshape.163
  208.5 4.9 %add_convert_fusion.1 = bf16[768,1536]{1,0:T(8,128)(2,1)S(1)} fusion(f32[768,1536]{1,0:T(8,128)S(1)} %fusion.15, bf16[768,1024]{1,0:T(8,128)(2,1)S(1)} %get-tuple-element.31, bf16[1,3584,1024]{2,1,0:T(8,128)(2,1)} %param.14), kind=kOutput, calls=%fused_computation.10 | convolution fusion | flops 2418278400 | bytes 11796480 | tf_op jit(solution)/shard_map/dot_general | solution.py:8
  213.4 0.2 fusion.22
  213.6 4.2 %reshape.159 = bf16[128,78,128]{2,1,0:T(8,128)(2,1)} reshape(bf16[768,1664]{1,0:T(8,128)(2,1)S(1)} %fusion.22) | data formatting | bytes 5111808 | tf_op jit(solution)/shard_map/reshape | solution.py:49
  217.7 7.5 %all-to-all-start.2 = ((bf16[128,78,128]{2,1,0:T(8,128)(2,1)}), bf16[128,78,128]{2,1,0:T(8,128)(2,1)S(1)}, u32[]{:S(2)}, u32[]{:S(2)}) async-start(bf16[128,78,128]{2,1,0:T(8,128)(2,1)} %reshape.159), calls=%async_computation.2 | async-start | bytes 5242880 | tf_op jit(solution)/shard_map/all_to_all | solution.py:50
  225.2 0.0 copy-start.9
  225.2 5.9 %fusion.8 = f32[768,2048]{1,0:T(8,128)S(1)} fusion(bf16[768,1024]{1,0:T(8,128)(2,1)} %copy-done.10, bf16[1,3584,1024]{2,1,0:T(8,128)(2,1)} %param.14), kind=kOutput, calls=%fused_computation.11 | convolution fusion | flops 3221225472 | bytes 12058624 | tf_op jit(solution)/shard_map/dot_general | solution.py:8
  231.1 0.0 copy-done.9
  231.1 7.0 %add_convert_fusion = bf16[768,2048]{1,0:T(8,128)(2,1)} fusion(f32[768,2048]{1,0:T(8,128)S(1)} %fusion.8, bf16[768,1024]{1,0:T(8,128)(2,1)S(1)} %copy-done.9, bf16[1,3584,1024]{2,1,0:T(8,128)(2,1)} %param.13), kind=kOutput, calls=%fused_computation.6 | convolution fusion | flops 3224371200 | bytes 15204352 | tf_op jit(solution)/shard_map/dot_general | solution.py:8
  238.1 5.9 %reshape.161 = bf16[128,96,128]{2,1,0:T(8,128)(2,1)} reshape(bf16[768,2048]{1,0:T(8,128)(2,1)} %add_convert_fusion) | data formatting | bytes 6291456 | tf_op jit(solution)/shard_map/reshape | solution.py:49
  244.0 16.9 %all-to-all-done.2 = bf16[128,78,128]{2,1,0:T(8,128)(2,1)S(1)} async-done(((bf16[128,78,128]{2,1,0:T(8,128)(2,1)}), bf16[128,78,128]{2,1,0:T(8,128)(2,1)S(1)}, u32[]{:S(2)}, u32[]{:S(2)}) %all-to-all-start.2) | async-done | bytes 2555936 | tf_op jit(solution)/shard_map/all_to_all | solution.py:50
  261.0 5.8 %all-to-all-start.3 = ((bf16[128,96,128]{2,1,0:T(8,128)(2,1)}), bf16[128,96,128]{2,1,0:T(8,128)(2,1)}, u32[]{:S(2)}, u32[]{:S(2)}) async-start(bf16[128,96,128]{2,1,0:T(8,128)(2,1)} %reshape.161), calls=%async_computation.3 | async-start | bytes 6291456 | tf_op jit(solution)/shard_map/all_to_all | solution.py:50
  266.8 0.0 copy-start.4
  266.8 3.9 %reshape.160 = bf16[768,1664]{1,0:T(8,128)(2,1)} reshape(bf16[128,78,128]{2,1,0:T(8,128)(2,1)S(1)} %all-to-all-done.2) | data formatting | bytes 5111808 | tf_op jit(solution)/shard_map/reshape | solution.py:51
  270.7 1.3 fusion.25
  272.1 0.1 convert_element_type.60
  272.2 0.7 copy.34
  272.9 0.0 copy-done.4
  272.9 2.2 convolution_convert_fusion.1
  275.1 0.0 copy-start.5
  275.1 33.0 %all-to-all-done.3 = bf16[128,96,128]{2,1,0:T(8,128)(2,1)} async-done(((bf16[128,96,128]{2,1,0:T(8,128)(2,1)}), bf16[128,96,128]{2,1,0:T(8,128)(2,1)}, u32[]{:S(2)}, u32[]{:S(2)}) %all-to-all-start.3) | async-done | bytes 3145760 | tf_op jit(solution)/shard_map/all_to_all | solution.py:50
  308.0 5.9 %reshape.162 = bf16[768,2048]{1,0:T(8,128)(2,1)} reshape(bf16[128,96,128]{2,1,0:T(8,128)(2,1)} %all-to-all-done.3) | data formatting | bytes 6291456 | tf_op jit(solution)/shard_map/reshape | solution.py:51
  313.9 0.0 copy-done.5
  313.9 2.5 convolution_convert_fusion
  316.4 1.0 pad_maximum_fusion
  (18 shorter events, 0.1 us)
Async XLA Ops:
  0.6 3.0 copy-start
  3.6 27.3 %copy-start.3 = (pred[768,128]{1,0:T(8,128)(4,1)}, pred[768,128]{1,0:T(8,128)(4,1)S(1)}, u32[]{:S(2)}) copy-start(pred[768,128]{1,0:T(8,128)(4,1)S(1)} %fusion.24) | copy-start | bytes 294916
  18.7 12.0 %copy-start.7 = (bf16[128,4]{0,1:T(4,128)(2,1)S(1)}, bf16[128,4]{0,1:T(4,128)(2,1)}, u32[]{:S(2)}) copy-start(bf16[128,4]{0,1:T(4,128)(2,1)} %param.12) | copy-start | bytes 3076
  18.7 12.2 %copy-start.6 = (bf16[128,3584]{1,0:T(8,128)(2,1)S(1)}, bf16[128,3584]{1,0:T(8,128)(2,1)}, u32[]{:S(2)}) copy-start(bf16[128,3584]{1,0:T(8,128)(2,1)} %param.10) | copy-start | bytes 2752516
  18.7 80.4 %all-to-all-start.1 = ((bf16[128,168,128]{2,1,0:T(8,128)(2,1)}), bf16[128,168,128]{2,1,0:T(8,128)(2,1)}, u32[]{:S(2)}, u32[]{:S(2)}) async-start(bf16[128,168,128]{2,1,0:T(8,128)(2,1)} %reshape.156), calls=%async_computation.1 | async-start | bytes 11010048 | tf_op jit(solution)/shard_map/all_to_all | solution.py:50
  99.2 78.3 %all-to-all-start = ((bf16[128,174,128]{2,1,0:T(8,128)(2,1)}), bf16[128,174,128]{2,1,0:T(8,128)(2,1)}, u32[]{:S(2)}, u32[]{:S(2)}) async-start(bf16[128,174,128]{2,1,0:T(8,128)(2,1)} %reshape.154), calls=%async_computation | async-start | bytes 11534336 | tf_op jit(solution)/shard_map/all_to_all | solution.py:50
  118.2 10.6 %copy-start.2 = (bf16[768,3584]{1,0:T(8,128)(2,1)S(1)}, bf16[768,3584]{1,0:T(8,128)(2,1)}, u32[]{:S(2)}) copy-start(bf16[768,3584]{1,0:T(8,128)(2,1)} %reshape.157) | copy-start | bytes 16515076
  201.9 5.7 %copy-start.8 = (bf16[768,1024]{1,0:T(8,128)(2,1)}, bf16[768,1024]{1,0:T(8,128)(2,1)S(1)}, u32[]{:S(2)}) copy-start(bf16[768,1024]{1,0:T(8,128)(2,1)S(1)} %get-tuple-element.30) | copy-start | bytes 4718596
  201.9 6.6 %copy-start.10 = (bf16[768,1024]{1,0:T(8,128)(2,1)}, bf16[768,1024]{1,0:T(8,128)(2,1)S(1)}, u32[]{:S(2)}) copy-start(bf16[768,1024]{1,0:T(8,128)(2,1)S(1)} %get-tuple-element.31) | copy-start | bytes 4718596
  217.7 43.2 %all-to-all-start.2 = ((bf16[128,78,128]{2,1,0:T(8,128)(2,1)}), bf16[128,78,128]{2,1,0:T(8,128)(2,1)S(1)}, u32[]{:S(2)}, u32[]{:S(2)}) async-start(bf16[128,78,128]{2,1,0:T(8,128)(2,1)} %reshape.159), calls=%async_computation.2 | async-start | bytes 5242880 | tf_op jit(solution)/shard_map/all_to_all | solution.py:50
  225.2 5.9 %copy-start.9 = (bf16[768,1024]{1,0:T(8,128)(2,1)S(1)}, bf16[768,1024]{1,0:T(8,128)(2,1)}, u32[]{:S(2)}) copy-start(bf16[768,1024]{1,0:T(8,128)(2,1)} %copy-done.8) | copy-start | bytes 4718596
  261.0 47.1 %all-to-all-start.3 = ((bf16[128,96,128]{2,1,0:T(8,128)(2,1)}), bf16[128,96,128]{2,1,0:T(8,128)(2,1)}, u32[]{:S(2)}, u32[]{:S(2)}) async-start(bf16[128,96,128]{2,1,0:T(8,128)(2,1)} %reshape.161), calls=%async_computation.3 | async-start | bytes 6291456 | tf_op jit(solution)/shard_map/all_to_all | solution.py:50
  266.8 6.1 %copy-start.4 = (pred[768,128]{1,0:T(8,128)(4,1)S(1)}, pred[768,128]{1,0:T(8,128)(4,1)}, u32[]{:S(2)}) copy-start(pred[768,128]{1,0:T(8,128)(4,1)} %copy-done.3) | copy-start | bytes 294916
  275.1 38.9 %copy-start.5 = (pred[768,128]{1,0:T(8,128)(4,1)S(1)}, pred[768,128]{1,0:T(8,128)(4,1)}, u32[]{:S(2)}) copy-start(pred[768,128]{1,0:T(8,128)(4,1)} %copy-done.3) | copy-start | bytes 294916
  308.0 9.4 %copy-start.1 = (bf16[128,3584]{1,0:T(8,128)(2,1)S(1)}, bf16[128,3584]{1,0:T(8,128)(2,1)}, u32[]{:S(2)}) copy-start(bf16[128,3584]{1,0:T(8,128)(2,1)} %param.9) | copy-start | bytes 2752516

commit v3 on v2

--- a/solution.py
+++ b/solution.py
@@ -72,7 +72,7 @@
     grad_gate = (back_hidden * gate_factor).astype(jnp.bfloat16)
     grad_up = (back_hidden * active).astype(jnp.bfloat16)
 
-    half = model_width * 3 // 7 // (lane // 2) * (lane // 2)
+    half = model_width * 2 // 7 // (lane // 2) * (lane // 2)
     contrib_a = (_t_dot(grad_gate, gate_mat[:half]) + _t_dot(grad_up, up_mat[:half])).astype(
         jnp.bfloat16
     )

time: 319 us -> 319 us (level)
    all_to_all x4, waiting for transfers between devices: 140 us -> 137 us  [a2a(): lax.all_to_all(v, ('group', 'local'), split_axis=0, concat_axis=0, tiled=...]
  transfers between devices with their start and end apart: 4 -> 4, of which waited for: 4 -> 4; matrix products, arithmetic and copies ran while one was open for 24% -> 25% of each run, Pallas kernels for 0% -> 0%
where the time goes in v3:
time: 319 us; the launch traced here: 317 us
  waiting for transfers between devices  137 us (43%)
  matrix products  70.4 us (22%)
  local copies, waits for them, and re-layouts  70.3 us (22%)
  starting transfers between devices  33.5 us (11%)
  other arithmetic  5.44 us (2%)
    all_to_all x4, waiting for transfers between devices, a2a(): lax.all_to_all(v, ('group', 'local'), split_axis=0, concat_axis=0, tiled=...  137 us
    dot_general x5, matrix products, _t_dot(): lax.dot_general(a, b, (((1,), (1,)), ((), ())), preferred_element_type=jn...  34.9 us
    reshape x4, local copies, waits for them, and re-layouts, a2a(): v = v.reshape(expert_count, slot_cap * width // lane, lane)  34.4 us
    reshape x4, local copies, waits for them, and re-layouts, a2a(): return v.reshape(slot_total, width)  33.5 us
    all_to_all x4, starting transfers between devices, a2a(): lax.all_to_all(v, ('group', 'local'), split_axis=0, concat_axis=0, tiled=...  33.5 us
    dot_general x1, matrix products, local(): up_pre = jnp.dot(rows_x, up_mat, preferred_element_type=jnp.float32)  10.8 us
    dot_general x1, matrix products, local(): gate_pre = jnp.dot(rows_x, gate_mat, preferred_element_type=jnp.float32)  10.6 us
  transfers between devices with their start and end apart: 4, of which 4 were waited for; matrix products, arithmetic and copies ran while one was open for 25% of the time, Pallas kernels for 0%

profile of v3, /device:TPU:1, one launch (start us, length us, event | category | flops | bytes accessed | tf_op | source)
XLA Modules:
  0.0 317.2 jit_solution(3991578111487841450)
XLA Ops:
  0.6 0.0 copy-start
  0.6 0.9 copy.28
  1.5 0.1 eq.143
  1.6 0.1 eq.139
  1.7 0.1 copy.30
  1.8 0.2 fusion.37
  2.1 0.1 add_add_fusion
  2.2 0.2 fusion.36
  2.4 0.1 reduce_sum.30
  2.5 0.1 copy.32
  2.6 0.8 fusion.43
  3.4 0.2 fusion.23
  3.6 0.0 copy-done
  3.6 3.9 %fusion.44 = bf16[768,3584]{1,0:T(8,128)(2,1)} fusion(pred[768,128]{1,0:T(8,128)(4,1)S(1)} %fusion.23, bf16[128,3584]{1,0:T(8,128)(2,1)S(1)} %copy-done), kind=kOutput, calls=%fused_computation.83 | convolution fusion | flops 704643072 | bytes 6520832 | tf_op jit(solution)/shard_map/dot_general | solution.py:37
  7.6 11.1 %reshape.156 = bf16[128,168,128]{2,1,0:T(8,128)(2,1)} reshape(bf16[768,3584]{1,0:T(8,128)(2,1)} %fusion.44) | data formatting | bytes 11010048 | tf_op jit(solution)/shard_map/reshape | solution.py:49
  18.7 0.0 copy-start.4
  18.7 0.0 copy-start.3
  18.7 11.9 %all-to-all-start.1 = ((bf16[128,168,128]{2,1,0:T(8,128)(2,1)}), bf16[128,168,128]{2,1,0:T(8,128)(2,1)}, u32[]{:S(2)}, u32[]{:S(2)}) async-start(bf16[128,168,128]{2,1,0:T(8,128)(2,1)} %reshape.156), calls=%async_computation.1 | async-start | bytes 11010048 | tf_op jit(solution)/shard_map/all_to_all | solution.py:50
  30.7 0.0 copy-done.4
  30.7 0.2 select_select_fusion
  30.9 0.0 copy-done.3
  30.9 4.2 %fusion.30 = bf16[768,3712]{1,0:T(8,128)(2,1)} fusion(pred[768,128]{1,0:T(8,128)(4,1)S(1)} %fusion.23, bf16[128,128]{1,0:T(8,128)(2,1)S(1)} %select_select_fusion, bf16[128,3584]{1,0:T(8,128)(2,1)S(1)} %copy-done.3), kind=kOutput, calls=%fused_computation.38 | convolution fusion | flops 731709440 | bytes 6750208 | tf_op jit(solution)/shard_map/dot_general | solution.py:43
  35.1 11.9 %reshape.154 = bf16[128,174,128]{2,1,0:T(8,128)(2,1)} reshape(bf16[768,3712]{1,0:T(8,128)(2,1)} %fusion.30) | data formatting | bytes 11403264 | tf_op jit(solution)/shard_map/reshape | solution.py:49
  47.0 52.1 %all-to-all-done.1 = bf16[128,168,128]{2,1,0:T(8,128)(2,1)} async-done(((bf16[128,168,128]{2,1,0:T(8,128)(2,1)}), bf16[128,168,128]{2,1,0:T(8,128)(2,1)}, u32[]{:S(2)}, u32[]{:S(2)}) %all-to-all-start.1) | async-done | bytes 5505056 | tf_op jit(solution)/shard_map/all_to_all | solution.py:50
  99.1 7.8 %all-to-all-start = ((bf16[128,174,128]{2,1,0:T(8,128)(2,1)}), bf16[128,174,128]{2,1,0:T(8,128)(2,1)}, u32[]{:S(2)}, u32[]{:S(2)}) async-start(bf16[128,174,128]{2,1,0:T(8,128)(2,1)} %reshape.154), calls=%async_computation | async-start | bytes 11534336 | tf_op jit(solution)/shard_map/all_to_all | solution.py:50
  106.9 0.6 compare_reduce_fusion
  107.5 10.6 %reshape.157 = bf16[768,3584]{1,0:T(8,128)(2,1)} reshape(bf16[128,168,128]{2,1,0:T(8,128)(2,1)} %all-to-all-done.1) | data formatting | bytes 11010048 | tf_op jit(solution)/shard_map/reshape | solution.py:51
  118.2 0.0 copy-start.2
  118.2 10.6 %fusion = f32[768,1024]{1,0:T(8,128)S(1)} fusion(bf16[768,3584]{1,0:T(8,128)(2,1)} %reshape.157, bf16[1,3584,1024]{2,1,0:T(8,128)(2,1)} %param.13), kind=kOutput, calls=%fused_computation.1 | convolution fusion | flops 5637144576 | bytes 15990784 | tf_op jit(solution)/shard_map/dot_general | solution.py:54
  128.8 0.0 copy-done.2
  128.8 10.8 %multiply_convert_fusion.2 = (bf16[768,1024]{1,0:T(8,128)(2,1)S(1)}, f32[768,1024]{1,0:T(8,128)}, f32[768,1024]{1,0:T(8,128)}) fusion(f32[768,1024]{1,0:T(8,128)S(1)} %fusion, bf16[768,3584]{1,0:T(8,128)(2,1)S(1)} %copy-done.2, bf16[1,3584,1024]{2,1,0:T(8,128)(2,1)} %param.14), kind=kOutput, calls=%fused_computation.20 | convolution fusion | flops 5645795328 | bytes 23855104 | tf_op jit(solution)/shard_map/dot_general | solution.py:55
  139.6 37.9 %all-to-all-done = bf16[128,174,128]{2,1,0:T(8,128)(2,1)} async-done(((bf16[128,174,128]{2,1,0:T(8,128)(2,1)}), bf16[128,174,128]{2,1,0:T(8,128)(2,1)}, u32[]{:S(2)}, u32[]{:S(2)}) %all-to-all-start) | async-done | bytes 5701664 | tf_op jit(solution)/shard_map/all_to_all | solution.py:50
  177.4 11.5 %reshape.155 = bf16[768,3712]{1,0:T(8,128)(2,1)} reshape(bf16[128,174,128]{2,1,0:T(8,128)(2,1)} %all-to-all-done) | data formatting | bytes 11403264 | tf_op jit(solution)/shard_map/reshape | solution.py:51
  189.0 1.0 slice_convert_fusion
  189.9 0.3 fusion.35
  190.2 11.6 %multiply_convert_fusion = (bf16[768,1024]{1,0:T(8,128)(2,1)S(1)}, bf16[768,1024]{1,0:T(8,128)(2,1)S(1)}, bf16[768]{0:T(1024)(128)(2,1)S(1)}) fusion(f32[768,1024]{1,0:T(8,128)} %get-tuple-element.18, f32[768]{0:T(1024)S(1)} %fusion.35, f32[768,1024]{1,0:T(8,128)} %get-tuple-element.17, bf16[768,1024]{1,0:T(8,128)(2,1)S(1)} %get-tuple-element.19, ...), kind=kOutput, calls=%fused_computation.18 | convolution fusion | flops 5643435008 | bytes 23859712 | tf_op jit(solution)/shard_map/dot_general | solution.py:8
  201.9 0.0 copy-start.6
  201.9 0.0 copy-start.5
  201.9 4.6 %fusion.14 = f32[768,1024]{1,0:T(8,128)S(1)} fusion(bf16[768,1024]{1,0:T(8,128)(2,1)S(1)} %get-tuple-element.30, bf16[1,3584,1024]{2,1,0:T(8,128)(2,1)} %param.14), kind=kOutput, calls=%fused_computation.24 | convolution fusion | flops 1610612736 | bytes 6815744 | tf_op jit(solution)/shard_map/dot_general | solution.py:8
  206.5 0.0 copy-done.6
  206.5 0.7 convert_select_fusion
  207.1 0.2 reshape.163
  207.3 0.0 copy-done.5
  207.3 3.5 %add_convert_fusion.1 = bf16[768,1024]{1,0:T(8,128)(2,1)S(1)} fusion(f32[768,1024]{1,0:T(8,128)S(1)} %fusion.14, bf16[768,1024]{1,0:T(8,128)(2,1)S(1)} %get-tuple-element.31, bf16[1,3584,1024]{2,1,0:T(8,128)(2,1)} %param.13), kind=kOutput, calls=%fused_computation.17 | convolution fusion | flops 1612185600 | bytes 8388608 | tf_op jit(solution)/shard_map/dot_general | solution.py:8
  210.8 0.1 fusion.20
  211.0 3.0 reshape.159
  213.9 7.5 %all-to-all-start.2 = ((bf16[128,54,128]{2,1,0:T(8,128)(2,1)}), bf16[128,54,128]{2,1,0:T(8,128)(2,1)S(1)}, u32[]{:S(2)}, u32[]{:S(2)}) async-start(bf16[128,54,128]{2,1,0:T(8,128)(2,1)} %reshape.159), calls=%async_computation.2 | async-start | bytes 3670016 | tf_op jit(solution)/shard_map/all_to_all | solution.py:50
  221.4 0.0 copy-start.7
  221.4 6.8 %fusion.8 = f32[768,2560]{1,0:T(8,128)S(1)} fusion(bf16[768,1024]{1,0:T(8,128)(2,1)} %copy-done.5, bf16[1,3584,1024]{2,1,0:T(8,128)(2,1)} %param.13), kind=kOutput, calls=%fused_computation.9 | convolution fusion | flops 4026531840 | bytes 14680064 | tf_op jit(solution)/shard_map/dot_general | solution.py:8
  228.2 0.0 copy-done.7
  228.2 8.4 %add_convert_fusion = bf16[768,2560]{1,0:T(8,128)(2,1)} fusion(f32[768,2560]{1,0:T(8,128)S(1)} %fusion.8, bf16[768,1024]{1,0:T(8,128)(2,1)S(1)} %copy-done.7, bf16[1,3584,1024]{2,1,0:T(8,128)(2,1)} %param.14), kind=kOutput, calls=%fused_computation | convolution fusion | flops 4030464000 | bytes 18612224 | tf_op jit(solution)/shard_map/dot_general | solution.py:8
  236.6 8.4 %reshape.161 = bf16[128,120,128]{2,1,0:T(8,128)(2,1)} reshape(bf16[768,2560]{1,0:T(8,128)(2,1)} %add_convert_fusion) | data formatting | bytes 7864320 | tf_op jit(solution)/shard_map/reshape | solution.py:49
  245.0 3.8 %all-to-all-done.2 = bf16[128,54,128]{2,1,0:T(8,128)(2,1)S(1)} async-done(((bf16[128,54,128]{2,1,0:T(8,128)(2,1)}), bf16[128,54,128]{2,1,0:T(8,128)(2,1)S(1)}, u32[]{:S(2)}, u32[]{:S(2)}) %all-to-all-start.2) | async-done | bytes 1769504 | tf_op jit(solution)/shard_map/all_to_all | solution.py:50
  248.9 6.3 %all-to-all-start.3 = ((bf16[128,120,128]{2,1,0:T(8,128)(2,1)}), bf16[128,120,128]{2,1,0:T(8,128)(2,1)}, u32[]{:S(2)}, u32[]{:S(2)}) async-start(bf16[128,120,128]{2,1,0:T(8,128)(2,1)} %reshape.161), calls=%async_computation.3 | async-start | bytes 7864320 | tf_op jit(solution)/shard_map/all_to_all | solution.py:50
  255.2 3.0 reshape.160
  258.3 1.3 fusion.24
  259.6 0.1 convert_element_type.60
  259.8 0.7 copy.34
  260.4 1.8 fusion.27
  262.2 42.8 %all-to-all-done.3 = bf16[128,120,128]{2,1,0:T(8,128)(2,1)} async-done(((bf16[128,120,128]{2,1,0:T(8,128)(2,1)}), bf16[128,120,128]{2,1,0:T(8,128)(2,1)}, u32[]{:S(2)}, u32[]{:S(2)}) %all-to-all-start.3) | async-done | bytes 3932192 | tf_op jit(solution)/shard_map/all_to_all | solution.py:50
  305.1 8.3 %reshape.162 = bf16[768,2560]{1,0:T(8,128)(2,1)} reshape(bf16[128,120,128]{2,1,0:T(8,128)(2,1)} %all-to-all-done.3) | data formatting | bytes 7864320 | tf_op jit(solution)/shard_map/reshape | solution.py:51
  313.4 2.8 convolution_convert_fusion
  316.2 1.0 pad_maximum_fusion
  317.2 0.0 copy-done.1
  (12 shorter events, 0.1 us)
Async XLA Ops:
  0.6 3.0 copy-start
  18.7 12.0 %copy-start.4 = (bf16[128,4]{0,1:T(4,128)(2,1)S(1)}, bf16[128,4]{0,1:T(4,128)(2,1)}, u32[]{:S(2)}) copy-start(bf16[128,4]{0,1:T(4,128)(2,1)} %param.12) | copy-start | bytes 3076
  18.7 12.2 %copy-start.3 = (bf16[128,3584]{1,0:T(8,128)(2,1)S(1)}, bf16[128,3584]{1,0:T(8,128)(2,1)}, u32[]{:S(2)}) copy-start(bf16[128,3584]{1,0:T(8,128)(2,1)} %param.10) | copy-start | bytes 2752516
  18.7 80.4 %all-to-all-start.1 = ((bf16[128,168,128]{2,1,0:T(8,128)(2,1)}), bf16[128,168,128]{2,1,0:T(8,128)(2,1)}, u32[]{:S(2)}, u32[]{:S(2)}) async-start(bf16[128,168,128]{2,1,0:T(8,128)(2,1)} %reshape.156), calls=%async_computation.1 | async-start | bytes 11010048 | tf_op jit(solution)/shard_map/all_to_all | solution.py:50
  99.1 78.3 %all-to-all-start = ((bf16[128,174,128]{2,1,0:T(8,128)(2,1)}), bf16[128,174,128]{2,1,0:T(8,128)(2,1)}, u32[]{:S(2)}, u32[]{:S(2)}) async-start(bf16[128,174,128]{2,1,0:T(8,128)(2,1)} %reshape.154), calls=%async_computation | async-start | bytes 11534336 | tf_op jit(solution)/shard_map/all_to_all | solution.py:50
  118.2 10.6 %copy-start.2 = (bf16[768,3584]{1,0:T(8,128)(2,1)S(1)}, bf16[768,3584]{1,0:T(8,128)(2,1)}, u32[]{:S(2)}) copy-start(bf16[768,3584]{1,0:T(8,128)(2,1)} %reshape.157) | copy-start | bytes 16515076
  201.9 4.6 %copy-start.6 = (bf16[768,1024]{1,0:T(8,128)(2,1)}, bf16[768,1024]{1,0:T(8,128)(2,1)S(1)}, u32[]{:S(2)}) copy-start(bf16[768,1024]{1,0:T(8,128)(2,1)S(1)} %get-tuple-element.30) | copy-start | bytes 4718596
  201.9 5.4 %copy-start.5 = (bf16[768,1024]{1,0:T(8,128)(2,1)}, bf16[768,1024]{1,0:T(8,128)(2,1)S(1)}, u32[]{:S(2)}) copy-start(bf16[768,1024]{1,0:T(8,128)(2,1)S(1)} %get-tuple-element.31) | copy-start | bytes 4718596
  213.9 34.9 %all-to-all-start.2 = ((bf16[128,54,128]{2,1,0:T(8,128)(2,1)}), bf16[128,54,128]{2,1,0:T(8,128)(2,1)S(1)}, u32[]{:S(2)}, u32[]{:S(2)}) async-start(bf16[128,54,128]{2,1,0:T(8,128)(2,1)} %reshape.159), calls=%async_computation.2 | async-start | bytes 3670016 | tf_op jit(solution)/shard_map/all_to_all | solution.py:50
  221.4 6.8 %copy-start.7 = (bf16[768,1024]{1,0:T(8,128)(2,1)S(1)}, bf16[768,1024]{1,0:T(8,128)(2,1)}, u32[]{:S(2)}) copy-start(bf16[768,1024]{1,0:T(8,128)(2,1)} %copy-done.6) | copy-start | bytes 4718596
  248.9 56.2 %all-to-all-start.3 = ((bf16[128,120,128]{2,1,0:T(8,128)(2,1)}), bf16[128,120,128]{2,1,0:T(8,128)(2,1)}, u32[]{:S(2)}, u32[]{:S(2)}) async-start(bf16[128,120,128]{2,1,0:T(8,128)(2,1)} %reshape.161), calls=%async_computation.3 | async-start | bytes 7864320 | tf_op jit(solution)/shard_map/all_to_all | solution.py:50
  305.1 12.1 %copy-start.1 = (bf16[128,3584]{1,0:T(8,128)(2,1)S(1)}, bf16[128,3584]{1,0:T(8,128)(2,1)}, u32[]{:S(2)}) copy-start(bf16[128,3584]{1,0:T(8,128)(2,1)} %param.9) | copy-start | bytes 2752516

commit v4 on v3

--- a/solution.py
+++ b/solution.py
@@ -34,15 +34,15 @@
     sel_a = sel.astype(jnp.bfloat16)
     sel_t = jnp.any(sel.reshape(slot_total, token_rows, top_count), axis=2).astype(jnp.bfloat16)
 
-    send_x = jnp.dot(sel_t, tokens, preferred_element_type=jnp.bfloat16)
     cols = jnp.arange(lane, dtype=jnp.int32)[None, :]
     info = jnp.zeros((token_rows, lane), jnp.bfloat16)
     for k in range(top_count):
         info = jnp.where(cols == k, combine[:, k : k + 1], info)
         info = jnp.where(cols == top_count + k, expert_ids[:, k : k + 1].astype(jnp.bfloat16), info)
-    send_dyp = jnp.dot(
-        sel_t, jnp.concatenate([grad_out, info], axis=1), preferred_element_type=jnp.bfloat16
+    send_x = jnp.dot(
+        sel_t, jnp.concatenate([tokens, info], axis=1), preferred_element_type=jnp.bfloat16
     )
+    send_dy = jnp.dot(sel_t, grad_out, preferred_element_type=jnp.bfloat16)
 
     def a2a(v):
         width = v.shape[-1]
@@ -50,22 +50,32 @@
         v = lax.all_to_all(v, ("group", "local"), split_axis=0, concat_axis=0, tiled=True)
         return v.reshape(slot_total, width)
 
-    rows_x = a2a(send_x)
+    info_width = model_width + lane
+    rows_xi = lax.all_to_all(
+        send_x.reshape(expert_count, slot_cap * info_width // lane, lane),
+        ("group", "local"), split_axis=0, concat_axis=0, tiled=True,
+    )
+    send_dy = send_dy.reshape(expert_count, slot_cap * model_width // lane, lane)
+    rows_xi, send_dy = lax.optimization_barrier((rows_xi, send_dy))
+    rows_xi = rows_xi.reshape(slot_total, info_width)
+    rows_x = rows_xi[:, :model_width]
+    e_me = (lax.axis_index("group") * local_count + lax.axis_index("local")).astype(jnp.float32)
+    info_rows = rows_xi[:, model_width : model_width + 2 * top_count].astype(jnp.float32)
+    rows_p = jnp.sum(
+        jnp.where(info_rows[:, top_count:] == e_me, info_rows[:, :top_count], 0.0), axis=1
+    )
     gate_pre = jnp.dot(rows_x, gate_mat, preferred_element_type=jnp.float32)
     up_pre = jnp.dot(rows_x, up_mat, preferred_element_type=jnp.float32)
     sigmoid_gate = jax.nn.sigmoid(gate_pre)
     active = gate_pre * sigmoid_gate
     hidden = (active * up_pre).astype(jnp.bfloat16)
     gate_factor = up_pre * sigmoid_gate * (1.0 + gate_pre * (1.0 - sigmoid_gate))
-    gate_factor, active, hidden = lax.optimization_barrier((gate_factor, active, hidden))
+    gate_factor, active, hidden, rows_p = lax.optimization_barrier(
+        (gate_factor, active, hidden, rows_p)
+    )
 
-    rows_dyp = a2a(send_dyp)
-    rows_dy = rows_dyp[:, :model_width]
-    e_me = (lax.axis_index("group") * local_count + lax.axis_index("local")).astype(jnp.float32)
-    info_rows = rows_dyp[:, model_width : model_width + 2 * top_count].astype(jnp.float32)
-    rows_p = jnp.sum(
-        jnp.where(info_rows[:, top_count:] == e_me, info_rows[:, :top_count], 0.0), axis=1
-    )
+    rows_dy = lax.all_to_all(send_dy, ("group", "local"), split_axis=0, concat_axis=0, tiled=True)
+    rows_dy = rows_dy.reshape(slot_total, model_width)
     back_raw = _t_dot(rows_dy, down_mat)
     grad_weight = jnp.sum(hidden.astype(jnp.float32) * back_raw, axis=1).astype(jnp.bfloat16)
     back_hidden = back_raw * rows_p[:, None]

time: 319 us -> 320 us (level)
    all_to_all x0 -> x2, waiting for transfers between devices: none -> 91.7 us  [the longest x1 55.4 us: local(): lax.all_to_all(send_x.reshape(expert_count, slot_cap * info_width // lane...]
    all_to_all x4 -> x2, waiting for transfers between devices: 137 us -> 46.6 us  [a2a(): lax.all_to_all(v, ('group', 'local'), split_axis=0, concat_axis=0, tiled=...]
    reshape x0 -> x4, local copies, waits for them, and re-layouts: none -> 45.2 us  [the longest x1 11.9 us: local(): send_x.reshape(expert_count, slot_cap * info_width // lane, lane)]
    reshape x4 -> x2, local copies, waits for them, and re-layouts: 34.4 us -> 11.5 us  [a2a(): v = v.reshape(expert_count, slot_cap * width // lane, lane)]
    reshape x4 -> x2, local copies, waits for them, and re-layouts: 33.5 us -> 11.3 us  [a2a(): return v.reshape(slot_total, width)]
    all_to_all x0 -> x2, starting transfers between devices: none -> 19.8 us  [the longest x1 11.9 us: local(): lax.all_to_all(send_x.reshape(expert_count, slot_cap * info_width // lane...]
    all_to_all x4 -> x2, starting transfers between devices: 33.5 us -> 13.8 us  [a2a(): lax.all_to_all(v, ('group', 'local'), split_axis=0, concat_axis=0, tiled=...]
where the time goes in v4:
time: 320 us; the launch traced here: 318 us
  waiting for transfers between devices  138 us (43%)
  local copies, waits for them, and re-layouts  71.3 us (22%)
  matrix products  67.8 us (21%)
  starting transfers between devices  33.6 us (10%)
  other arithmetic  5.63 us (2%)
    all_to_all x1, waiting for transfers between devices, local(): lax.all_to_all(send_x.reshape(expert_count, slot_cap * info_width // lane...  55.4 us
    all_to_all x2, waiting for transfers between devices, a2a(): lax.all_to_all(v, ('group', 'local'), split_axis=0, concat_axis=0, tiled=...  46.6 us
    all_to_all x1, waiting for transfers between devices, local(): lax.all_to_all(send_dy, ('group', 'local'), split_axis=0, concat_axis=0,...  36.3 us
    dot_general x5, matrix products, _t_dot(): lax.dot_general(a, b, (((1,), (1,)), ((), ())), preferred_element_type=jn...  34 us
    all_to_all x2, starting transfers between devices, a2a(): lax.all_to_all(v, ('group', 'local'), split_axis=0, concat_axis=0, tiled=...  13.8 us
    reshape x1, local copies, waits for them, and re-layouts, local(): send_x.reshape(expert_count, slot_cap * info_width // lane, lane)  11.9 us
    all_to_all x1, starting transfers between devices, local(): lax.all_to_all(send_x.reshape(expert_count, slot_cap * info_width // lane...  11.9 us
    reshape x2, local copies, waits for them, and re-layouts, a2a(): v = v.reshape(expert_count, slot_cap * width // lane, lane)  11.5 us
  transfers between devices with their start and end apart: 4, of which 4 were waited for; matrix products, arithmetic and copies ran while one was open for 25% of the time, Pallas kernels for 0%

profile of v4, /device:TPU:1, one launch (start us, length us, event | category | flops | bytes accessed | tf_op | source)
XLA Modules:
  0.0 317.5 jit_solution(943677716379889023)
XLA Ops:
  0.6 0.0 copy-start
  0.7 0.9 copy.28
  1.6 0.1 eq.139
  1.7 0.1 eq.143
  1.8 0.1 copy.30
  1.9 0.2 fusion.38
  2.1 0.1 add_add_fusion
  2.2 0.2 fusion.37
  2.5 0.1 reduce_sum.30
  2.6 0.1 copy.32
  2.7 0.8 fusion.44
  3.4 0.2 fusion.24
  3.7 0.8 slice_bitcast_fusion.7
  4.5 0.2 select_select_fusion
  4.7 5.3 %fusion.31 = bf16[768,3712]{1,0:T(8,128)(2,1)} fusion(pred[768,128]{1,0:T(8,128)(4,1)S(1)} %fusion.24, bf16[128,128]{1,0:T(8,128)(2,1)S(1)} %select_select_fusion, bf16[128,3584]{1,0:T(8,128)(2,1)} %param.9), kind=kOutput, calls=%fused_computation.39 | convolution fusion | flops 731709440 | bytes 6750208 | tf_op jit(solution)/shard_map/dot_general | solution.py:42
  10.0 11.9 %reshape.154 = bf16[128,174,128]{2,1,0:T(8,128)(2,1)} reshape(bf16[768,3712]{1,0:T(8,128)(2,1)} %fusion.31) | data formatting | bytes 11403264 | tf_op jit(solution)/shard_map/reshape | solution.py:55
  21.9 11.9 %all-to-all-start = ((bf16[128,174,128]{2,1,0:T(8,128)(2,1)}), bf16[128,174,128]{2,1,0:T(8,128)(2,1)}, u32[]{:S(2)}, u32[]{:S(2)}) async-start(bf16[128,174,128]{2,1,0:T(8,128)(2,1)} %reshape.154), calls=%async_computation | async-start | bytes 11534336 | tf_op jit(solution)/shard_map/all_to_all | solution.py:54
  33.8 0.0 copy-done
  33.8 4.0 %fusion.45 = bf16[768,3584]{1,0:T(8,128)(2,1)} fusion(pred[768,128]{1,0:T(8,128)(4,1)S(1)} %fusion.24, bf16[128,3584]{1,0:T(8,128)(2,1)S(1)} %copy-done), kind=kOutput, calls=%fused_computation.84 | convolution fusion | flops 704643072 | bytes 6520832 | tf_op jit(solution)/shard_map/dot_general | solution.py:45
  37.8 11.1 %reshape.155 = bf16[128,168,128]{2,1,0:T(8,128)(2,1)} reshape(bf16[768,3584]{1,0:T(8,128)(2,1)} %fusion.45) | data formatting | bytes 11010048 | tf_op jit(solution)/shard_map/reshape | solution.py:58
  49.0 55.4 %all-to-all-done = bf16[128,174,128]{2,1,0:T(8,128)(2,1)} async-done(((bf16[128,174,128]{2,1,0:T(8,128)(2,1)}), bf16[128,174,128]{2,1,0:T(8,128)(2,1)}, u32[]{:S(2)}, u32[]{:S(2)}) %all-to-all-start) | async-done | bytes 5701664 | tf_op jit(solution)/shard_map/all_to_all | solution.py:54
  104.3 7.9 %all-to-all-start.1 = ((bf16[128,168,128]{2,1,0:T(8,128)(2,1)}), bf16[128,168,128]{2,1,0:T(8,128)(2,1)}, u32[]{:S(2)}, u32[]{:S(2)}) async-start(bf16[128,168,128]{2,1,0:T(8,128)(2,1)} %reshape.155), calls=%async_computation.1 | async-start | bytes 11010048 | tf_op jit(solution)/shard_map/all_to_all | solution.py:77
  112.2 0.6 compare_reduce_fusion
  112.9 11.5 %reshape.157 = bf16[768,3712]{1,0:T(8,128)(2,1)} reshape(bf16[128,174,128]{2,1,0:T(8,128)(2,1)} %all-to-all-done) | data formatting | bytes 11403264 | tf_op jit(solution)/shard_map/reshape | solution.py:60
  124.4 1.1 slice_convert_fusion
  125.5 0.0 slice-start
  125.5 0.3 fusion.36
  125.8 0.0 slice-start.1
  125.8 0.0 slice-start.3
  125.9 10.1 %fusion = f32[768,1024]{1,0:T(8,128)S(1)} fusion(bf16[1,3584,1024]{2,1,0:T(8,128)(2,1)} %param.13, bf16[768,3712]{1,0:T(8,128)(2,1)} %reshape.157), kind=kOutput, calls=%fused_computation.1 | convolution fusion | flops 5637144576 | bytes 15990784 | tf_op jit(solution)/shard_map/dot_general | solution.py:67
  136.0 0.0 slice-done.2
  136.0 0.0 slice-done
  136.0 0.0 slice-done.1
  136.0 0.0 slice-done.3
  136.0 8.4 %multiply_convert_fusion.2 = (bf16[768,1024]{1,0:T(8,128)(2,1)S(1)}, f32[768,1024]{1,0:T(8,128)}, f32[768,1024]{1,0:T(8,128)}) fusion(f32[768,1024]{1,0:T(8,128)S(1)} %fusion, bf16[1,3584,1024]{2,1,0:T(8,128)(2,1)S(1)} %bitcast.65, bf16[768,3712]{1,0:T(8,128)(2,1)S(1)} %bitcast.63), kind=kOutput, calls=%fused_computation.21 | convolution fusion | flops 5645795328 | bytes 23855104 | tf_op jit(solution)/shard_map/dot_general | solution.py:68
  144.4 36.3 %all-to-all-done.1 = bf16[128,168,128]{2,1,0:T(8,128)(2,1)} async-done(((bf16[128,168,128]{2,1,0:T(8,128)(2,1)}), bf16[128,168,128]{2,1,0:T(8,128)(2,1)}, u32[]{:S(2)}, u32[]{:S(2)}) %all-to-all-start.1) | async-done | bytes 5505056 | tf_op jit(solution)/shard_map/all_to_all | solution.py:77
  180.7 10.6 %reshape.156 = bf16[768,3584]{1,0:T(8,128)(2,1)} reshape(bf16[128,168,128]{2,1,0:T(8,128)(2,1)} %all-to-all-done.1) | data formatting | bytes 11010048 | tf_op jit(solution)/shard_map/reshape | solution.py:78
  191.4 11.6 %multiply_convert_fusion = (bf16[768,1024]{1,0:T(8,128)(2,1)S(1)}, bf16[768,1024]{1,0:T(8,128)(2,1)S(1)}, bf16[768]{0:T(1024)(128)(2,1)S(1)}) fusion(f32[768,1024]{1,0:T(8,128)} %get-tuple-element.24, f32[768]{0:T(1024)S(1)} %fusion.36, f32[768,1024]{1,0:T(8,128)} %get-tuple-element.23, bf16[768,1024]{1,0:T(8,128)(2,1)S(1)} %get-tuple-element.25, ...), kind=kOutput, calls=%fused_computation.19 | convolution fusion | flops 5643435008 | bytes 23859712 | tf_op jit(solution)/shard_map/dot_general | solution.py:8
  203.0 0.0 copy-start.3
  203.0 0.0 copy-start.2
  203.0 0.7 convert_select_fusion
  203.7 0.2 reshape.163
  203.9 3.6 %fusion.15 = f32[768,1024]{1,0:T(8,128)S(1)} fusion(bf16[768,1024]{1,0:T(8,128)(2,1)S(1)} %get-tuple-element.36, bf16[1,3584,1024]{2,1,0:T(8,128)(2,1)} %param.14), kind=kOutput, calls=%fused_computation.25 | convolution fusion | flops 1610612736 | bytes 6815744 | tf_op jit(solution)/shard_map/dot_general | solution.py:8
  207.5 0.0 copy-done.3
  207.5 3.4 %add_convert_fusion.1 = bf16[768,1024]{1,0:T(8,128)(2,1)S(1)} fusion(f32[768,1024]{1,0:T(8,128)S(1)} %fusion.15, bf16[768,1024]{1,0:T(8,128)(2,1)S(1)} %get-tuple-element.37, bf16[1,3584,1024]{2,1,0:T(8,128)(2,1)} %param.13), kind=kOutput, calls=%fused_computation.18 | convolution fusion | flops 1612185600 | bytes 8388608 | tf_op jit(solution)/shard_map/dot_general | solution.py:8
  211.0 0.1 fusion.21
  211.1 3.1 reshape.159
  214.3 7.4 %all-to-all-start.2 = ((bf16[128,54,128]{2,1,0:T(8,128)(2,1)}), bf16[128,54,128]{2,1,0:T(8,128)(2,1)S(1)}, u32[]{:S(2)}, u32[]{:S(2)}) async-start(bf16[128,54,128]{2,1,0:T(8,128)(2,1)} %reshape.159), calls=%async_computation.2 | async-start | bytes 3670016 | tf_op jit(solution)/shard_map/all_to_all | solution.py:50
  221.6 0.0 copy-start.4
  221.6 6.8 %fusion.7 = f32[768,2560]{1,0:T(8,128)S(1)} fusion(bf16[768,1024]{1,0:T(8,128)(2,1)} %copy-done.2, bf16[1,3584,1024]{2,1,0:T(8,128)(2,1)} %param.13), kind=kOutput, calls=%fused_computation.8 | convolution fusion | flops 4026531840 | bytes 14680064 | tf_op jit(solution)/shard_map/dot_general | solution.py:8
  228.5 8.5 %add_convert_fusion = bf16[768,2560]{1,0:T(8,128)(2,1)} fusion(f32[768,2560]{1,0:T(8,128)S(1)} %fusion.7, bf16[768,1024]{1,0:T(8,128)(2,1)S(1)} %copy-done.4, bf16[1,3584,1024]{2,1,0:T(8,128)(2,1)} %param.14), kind=kOutput, calls=%fused_computation | convolution fusion | flops 4030464000 | bytes 18612224 | tf_op jit(solution)/shard_map/dot_general | solution.py:8
  236.9 8.4 %reshape.161 = bf16[128,120,128]{2,1,0:T(8,128)(2,1)} reshape(bf16[768,2560]{1,0:T(8,128)(2,1)} %add_convert_fusion) | data formatting | bytes 7864320 | tf_op jit(solution)/shard_map/reshape | solution.py:49
  245.4 3.7 %all-to-all-done.2 = bf16[128,54,128]{2,1,0:T(8,128)(2,1)S(1)} async-done(((bf16[128,54,128]{2,1,0:T(8,128)(2,1)}), bf16[128,54,128]{2,1,0:T(8,128)(2,1)S(1)}, u32[]{:S(2)}, u32[]{:S(2)}) %all-to-all-start.2) | async-done | bytes 1769504 | tf_op jit(solution)/shard_map/all_to_all | solution.py:50
  249.1 6.4 %all-to-all-start.3 = ((bf16[128,120,128]{2,1,0:T(8,128)(2,1)}), bf16[128,120,128]{2,1,0:T(8,128)(2,1)}, u32[]{:S(2)}, u32[]{:S(2)}) async-start(bf16[128,120,128]{2,1,0:T(8,128)(2,1)} %reshape.161), calls=%async_computation.3 | async-start | bytes 7864320 | tf_op jit(solution)/shard_map/all_to_all | solution.py:50
  255.5 3.0 reshape.160
  258.6 1.3 fusion.25
  260.0 0.1 convert_element_type.60
  260.1 0.7 copy.34
  260.7 1.8 fusion.28
  262.6 42.8 %all-to-all-done.3 = bf16[128,120,128]{2,1,0:T(8,128)(2,1)} async-done(((bf16[128,120,128]{2,1,0:T(8,128)(2,1)}), bf16[128,120,128]{2,1,0:T(8,128)(2,1)}, u32[]{:S(2)}, u32[]{:S(2)}) %all-to-all-start.3) | async-done | bytes 3932192 | tf_op jit(solution)/shard_map/all_to_all | solution.py:50
  305.4 8.3 %reshape.162 = bf16[768,2560]{1,0:T(8,128)(2,1)} reshape(bf16[128,120,128]{2,1,0:T(8,128)(2,1)} %all-to-all-done.3) | data formatting | bytes 7864320 | tf_op jit(solution)/shard_map/reshape | solution.py:51
  313.7 2.8 convolution_convert_fusion
  316.5 1.0 pad_maximum_fusion
  317.5 0.0 copy-done.1
  (16 shorter events, 0.1 us)
Async XLA Ops:
  0.6 33.2 %copy-start = (bf16[128,3584]{1,0:T(8,128)(2,1)S(1)}, bf16[128,3584]{1,0:T(8,128)(2,1)}, u32[]{:S(2)}) copy-start(bf16[128,3584]{1,0:T(8,128)(2,1)} %param.10) | copy-start | bytes 2752516
  21.9 82.5 %all-to-all-start = ((bf16[128,174,128]{2,1,0:T(8,128)(2,1)}), bf16[128,174,128]{2,1,0:T(8,128)(2,1)}, u32[]{:S(2)}, u32[]{:S(2)}) async-start(bf16[128,174,128]{2,1,0:T(8,128)(2,1)} %reshape.154), calls=%async_computation | async-start | bytes 11534336 | tf_op jit(solution)/shard_map/all_to_all | solution.py:54
  104.3 76.4 %all-to-all-start.1 = ((bf16[128,168,128]{2,1,0:T(8,128)(2,1)}), bf16[128,168,128]{2,1,0:T(8,128)(2,1)}, u32[]{:S(2)}, u32[]{:S(2)}) async-start(bf16[128,168,128]{2,1,0:T(8,128)(2,1)} %reshape.155), calls=%async_computation.1 | async-start | bytes 11010048 | tf_op jit(solution)/shard_map/all_to_all | solution.py:77
  124.4 11.5 %slice-start.2 = ((s8[7340032]{0:T(1024)(128)(4,1)}), s8[4194304]{0:T(1024)(128)(4,1)S(1)}, s32[]{:S(2)}) async-start(s8[7340032]{0:T(1024)(128)(4,1)} %bitcast.64), calls=%async_computation.6 | async-start | bytes 8388608
  125.5 10.4 %slice-start = ((s8[5701632]{0:T(1024)(128)(4,1)}), s8[4194304]{0:T(1024)(128)(4,1)S(1)}, s32[]{:S(2)}) async-start(s8[5701632]{0:T(1024)(128)(4,1)} %bitcast.62), calls=%async_computation.4 | async-start | bytes 8388608
  125.8 10.1 %slice-start.1 = ((s8[5701632]{0:T(1024)(128)(4,1)}), s8[1507328]{0:T(1024)(128)(4,1)S(1)}, s32[]{:S(2)}) async-start(s8[5701632]{0:T(1024)(128)(4,1)} %bitcast.62), calls=%async_computation.5 | async-start | bytes 3014656
  125.8 10.1 %slice-start.3 = ((s8[7340032]{0:T(1024)(128)(4,1)}), s8[3145728]{0:T(1024)(128)(4,1)S(1)}, s32[]{:S(2)}) async-start(s8[7340032]{0:T(1024)(128)(4,1)} %bitcast.64), calls=%async_computation.7 | async-start | bytes 6291456
  203.0 4.5 %copy-start.3 = (bf16[768,1024]{1,0:T(8,128)(2,1)}, bf16[768,1024]{1,0:T(8,128)(2,1)S(1)}, u32[]{:S(2)}) copy-start(bf16[768,1024]{1,0:T(8,128)(2,1)S(1)} %get-tuple-element.36) | copy-start | bytes 4718596
  203.0 4.5 %copy-start.2 = (bf16[768,1024]{1,0:T(8,128)(2,1)}, bf16[768,1024]{1,0:T(8,128)(2,1)S(1)}, u32[]{:S(2)}) copy-start(bf16[768,1024]{1,0:T(8,128)(2,1)S(1)} %get-tuple-element.37) | copy-start | bytes 4718596
  214.3 34.8 %all-to-all-start.2 = ((bf16[128,54,128]{2,1,0:T(8,128)(2,1)}), bf16[128,54,128]{2,1,0:T(8,128)(2,1)S(1)}, u32[]{:S(2)}, u32[]{:S(2)}) async-start(bf16[128,54,128]{2,1,0:T(8,128)(2,1)} %reshape.159), calls=%async_computation.2 | async-start | bytes 3670016 | tf_op jit(solution)/shard_map/all_to_all | solution.py:50
  221.6 6.8 %copy-start.4 = (bf16[768,1024]{1,0:T(8,128)(2,1)S(1)}, bf16[768,1024]{1,0:T(8,128)(2,1)}, u32[]{:S(2)}) copy-start(bf16[768,1024]{1,0:T(8,128)(2,1)} %copy-done.3) | copy-start | bytes 4718596
  249.1 56.3 %all-to-all-start.3 = ((bf16[128,120,128]{2,1,0:T(8,128)(2,1)}), bf16[128,120,128]{2,1,0:T(8,128)(2,1)}, u32[]{:S(2)}, u32[]{:S(2)}) async-start(bf16[128,120,128]{2,1,0:T(8,128)(2,1)} %reshape.161), calls=%async_computation.3 | async-start | bytes 7864320 | tf_op jit(solution)/shard_map/all_to_all | solution.py:50
  305.4 12.1 %copy-start.1 = (bf16[128,3584]{1,0:T(8,128)(2,1)S(1)}, bf16[128,3584]{1,0:T(8,128)(2,1)}, u32[]{:S(2)}) copy-start(bf16[128,3584]{1,0:T(8,128)(2,1)} %param.10) | copy-start | bytes 2752516

commit v5 on v0

--- a/solution.py
+++ b/solution.py
@@ -56,9 +56,8 @@
     sigmoid_gate = jax.nn.sigmoid(gate_pre)
     active = gate_pre * sigmoid_gate
     hidden = (active * up_pre).astype(jnp.bfloat16)
-    output = jnp.dot(hidden, down_mat, preferred_element_type=jnp.float32)
     gate_factor = up_pre * sigmoid_gate * (1.0 + gate_pre * (1.0 - sigmoid_gate))
-    gate_factor, active, output = lax.optimization_barrier((gate_factor, active, output))
+    gate_factor, active, hidden = lax.optimization_barrier((gate_factor, active, hidden))
 
     rows_dyp = a2a(send_dyp)
     rows_dy = rows_dyp[:, :model_width]
@@ -67,12 +66,13 @@
     rows_p = jnp.sum(
         jnp.where(info_rows[:, top_count:] == e_me, info_rows[:, :top_count], 0.0), axis=1
     )
-    back_hidden = _t_dot(rows_dy, down_mat)
-    back_hidden = back_hidden * rows_p[:, None]
+    back_raw = _t_dot(rows_dy, down_mat)
+    grad_weight = jnp.sum(hidden.astype(jnp.float32) * back_raw, axis=1).astype(jnp.bfloat16)
+    back_hidden = back_raw * rows_p[:, None]
     grad_gate = (back_hidden * gate_factor).astype(jnp.bfloat16)
     grad_up = (back_hidden * active).astype(jnp.bfloat16)
 
-    half = model_width // 2
+    half = model_width * 2 // 7 // (lane // 2) * (lane // 2)
     contrib_a = (_t_dot(grad_gate, gate_mat[:half]) + _t_dot(grad_up, up_mat[:half])).astype(
         jnp.bfloat16
     )
@@ -80,7 +80,6 @@
     contrib_b = (_t_dot(grad_gate, gate_mat[half:]) + _t_dot(grad_up, up_mat[half:])).astype(
         jnp.bfloat16
     )
-    grad_weight = jnp.sum(rows_dy.astype(jnp.float32) * output, axis=1).astype(jnp.bfloat16)
     gw_block = jnp.zeros((slot_total, lane), jnp.bfloat16).at[:, 0].set(grad_weight)
     back_b = a2a(jnp.concatenate([contrib_b, gw_block], axis=1))
 

time: 328 us -> 328 us (level)
  waiting for transfers between devices: 127 us -> 143 us
  other arithmetic: 14.1 us -> 7.41 us
  local copies, waits for them, and re-layouts: 73.5 us -> 68.4 us
  matrix products: 76.5 us -> 73.1 us
    all_to_all x4, waiting for transfers between devices: 127 us -> 143 us  [a2a(): lax.all_to_all(v, ('group', 'local'), split_axis=0, concat_axis=0, tiled=...]
    dot_general x1 -> x0, matrix products: 9.5 us -> none  [local(): output = jnp.dot(hidden, down_mat, preferred_element_type=jnp.float32)]
    reduce_sum x1 -> x0, other arithmetic: 6.99 us -> none  [local(): jnp.sum(rows_dy.astype(jnp.float32) * output, axis=1).astype(jnp.bfloat16)]
    dot_general x5, matrix products: 32.1 us -> 37.6 us  [_t_dot(): lax.dot_general(a, b, (((1,), (1,)), ((), ())), preferred_element_type=jn...]
  transfers between devices with their start and end apart: 4 -> 4, of which waited for: 4 -> 4; matrix products, arithmetic and copies ran while one was open for 28% -> 23% of each run, Pallas kernels for 0% -> 0%
where the time goes in v5:
time: 328 us; the launch traced here: 326 us
  waiting for transfers between devices  143 us (44%)
  matrix products  73.1 us (22%)
  local copies, waits for them, and re-layouts  68.4 us (21%)
  starting transfers between devices  33.5 us (10%)
  other arithmetic  7.41 us (2%)
    all_to_all x4, waiting for transfers between devices, a2a(): lax.all_to_all(v, ('group', 'local'), split_axis=0, concat_axis=0, tiled=...  143 us
    dot_general x5, matrix products, _t_dot(): lax.dot_general(a, b, (((1,), (1,)), ((), ())), preferred_element_type=jn...  37.6 us
    reshape x4, local copies, waits for them, and re-layouts, a2a(): v = v.reshape(expert_count, slot_cap * width // lane, lane)  33.5 us
    all_to_all x4, starting transfers between devices, a2a(): lax.all_to_all(v, ('group', 'local'), split_axis=0, concat_axis=0, tiled=...  33.5 us
    reshape x4, local copies, waits for them, and re-layouts, a2a(): return v.reshape(slot_total, width)  32.5 us
    dot_general x1, matrix products, local(): up_pre = jnp.dot(rows_x, up_mat, preferred_element_type=jnp.float32)  10.7 us
    dot_general x1, matrix products, local(): gate_pre = jnp.dot(rows_x, gate_mat, preferred_element_type=jnp.float32)  10.6 us
  transfers between devices with their start and end apart: 4, of which 4 were waited for; matrix products, arithmetic and copies ran while one was open for 23% of the time, Pallas kernels for 0%

profile of v5, /device:TPU:1, one launch (start us, length us, event | category | flops | bytes accessed | tf_op | source)
XLA Modules:
  0.0 325.8 jit_solution(17438645758833880578)
XLA Ops:
  0.6 0.0 copy-start
  0.6 0.9 copy.28
  1.5 0.1 eq.143
  1.6 0.1 eq.139
  1.7 0.1 copy.30
  1.8 0.2 fusion.37
  2.1 0.1 add_add_fusion
  2.2 0.2 fusion.36
  2.4 0.1 reduce_sum.30
  2.5 0.1 copy.32
  2.6 0.8 fusion.43
  3.4 0.2 fusion.26
  3.6 0.0 copy-done
  3.6 4.0 %fusion.44 = bf16[768,3584]{1,0:T(8,128)(2,1)} fusion(pred[768,128]{1,0:T(8,128)(4,1)S(1)} %fusion.26, bf16[128,3584]{1,0:T(8,128)(2,1)S(1)} %copy-done), kind=kOutput, calls=%fused_computation.83 | convolution fusion | flops 704643072 | bytes 6520832 | tf_op jit(solution)/shard_map/dot_general | solution.py:37
  7.6 11.1 %reshape.156 = bf16[128,168,128]{2,1,0:T(8,128)(2,1)} reshape(bf16[768,3584]{1,0:T(8,128)(2,1)} %fusion.44) | data formatting | bytes 11010048 | tf_op jit(solution)/shard_map/reshape | solution.py:49
  18.7 0.0 copy-start.4
  18.7 0.0 copy-start.3
  18.7 11.9 %all-to-all-start.1 = ((bf16[128,168,128]{2,1,0:T(8,128)(2,1)}), bf16[128,168,128]{2,1,0:T(8,128)(2,1)}, u32[]{:S(2)}, u32[]{:S(2)}) async-start(bf16[128,168,128]{2,1,0:T(8,128)(2,1)} %reshape.156), calls=%async_computation.1 | async-start | bytes 11010048 | tf_op jit(solution)/shard_map/all_to_all | solution.py:50
  30.7 0.0 copy-done.4
  30.7 0.2 select_select_fusion
  30.9 0.0 copy-done.3
  30.9 4.2 %fusion.30 = bf16[768,3712]{1,0:T(8,128)(2,1)} fusion(pred[768,128]{1,0:T(8,128)(4,1)S(1)} %fusion.26, bf16[128,128]{1,0:T(8,128)(2,1)S(1)} %select_select_fusion, bf16[128,3584]{1,0:T(8,128)(2,1)S(1)} %copy-done.3), kind=kOutput, calls=%fused_computation.38 | convolution fusion | flops 731709440 | bytes 6750208 | tf_op jit(solution)/shard_map/dot_general | solution.py:43
  35.1 11.9 %reshape.154 = bf16[128,174,128]{2,1,0:T(8,128)(2,1)} reshape(bf16[768,3712]{1,0:T(8,128)(2,1)} %fusion.30) | data formatting | bytes 11403264 | tf_op jit(solution)/shard_map/reshape | solution.py:49
  47.0 52.1 %all-to-all-done.1 = bf16[128,168,128]{2,1,0:T(8,128)(2,1)} async-done(((bf16[128,168,128]{2,1,0:T(8,128)(2,1)}), bf16[128,168,128]{2,1,0:T(8,128)(2,1)}, u32[]{:S(2)}, u32[]{:S(2)}) %all-to-all-start.1) | async-done | bytes 5505056 | tf_op jit(solution)/shard_map/all_to_all | solution.py:50
  99.1 7.8 %all-to-all-start = ((bf16[128,174,128]{2,1,0:T(8,128)(2,1)}), bf16[128,174,128]{2,1,0:T(8,128)(2,1)}, u32[]{:S(2)}, u32[]{:S(2)}) async-start(bf16[128,174,128]{2,1,0:T(8,128)(2,1)} %reshape.154), calls=%async_computation | async-start | bytes 11534336 | tf_op jit(solution)/shard_map/all_to_all | solution.py:50
  106.9 0.6 compare_reduce_fusion
  107.5 10.6 %reshape.157 = bf16[768,3584]{1,0:T(8,128)(2,1)} reshape(bf16[128,168,128]{2,1,0:T(8,128)(2,1)} %all-to-all-done.1) | data formatting | bytes 11010048 | tf_op jit(solution)/shard_map/reshape | solution.py:51
  118.2 0.0 copy-start.2
  118.2 10.6 %fusion.1 = f32[768,1024]{1,0:T(8,128)S(1)} fusion(bf16[768,3584]{1,0:T(8,128)(2,1)} %reshape.157, bf16[1,3584,1024]{2,1,0:T(8,128)(2,1)} %param.13), kind=kOutput, calls=%fused_computation.3 | convolution fusion | flops 5637144576 | bytes 15990784 | tf_op jit(solution)/shard_map/dot_general | solution.py:54
  128.8 0.0 copy-done.2
  128.8 10.7 %multiply_convert_fusion.2 = (bf16[768,1024]{1,0:T(8,128)(2,1)S(1)}, f32[768,1024]{1,0:T(8,128)}, f32[768,1024]{1,0:T(8,128)}) fusion(f32[768,1024]{1,0:T(8,128)S(1)} %fusion.1, bf16[768,3584]{1,0:T(8,128)(2,1)S(1)} %copy-done.2, bf16[1,3584,1024]{2,1,0:T(8,128)(2,1)} %param.14), kind=kOutput, calls=%fused_computation.23 | convolution fusion | flops 5645795328 | bytes 23855104 | tf_op jit(solution)/shard_map/dot_general | solution.py:55
  139.5 37.9 %all-to-all-done = bf16[128,174,128]{2,1,0:T(8,128)(2,1)} async-done(((bf16[128,174,128]{2,1,0:T(8,128)(2,1)}), bf16[128,174,128]{2,1,0:T(8,128)(2,1)}, u32[]{:S(2)}, u32[]{:S(2)}) %all-to-all-start) | async-done | bytes 5701664 | tf_op jit(solution)/shard_map/all_to_all | solution.py:50
  177.4 11.5 %reshape.155 = bf16[768,3712]{1,0:T(8,128)(2,1)} reshape(bf16[128,174,128]{2,1,0:T(8,128)(2,1)} %all-to-all-done) | data formatting | bytes 11403264 | tf_op jit(solution)/shard_map/reshape | solution.py:51
  189.0 1.0 slice_convert_fusion
  189.9 0.3 fusion.35
  190.2 11.6 %multiply_convert_fusion = (bf16[768,1024]{1,0:T(8,128)(2,1)S(1)}, bf16[768,1024]{1,0:T(8,128)(2,1)S(1)}, bf16[768]{0:T(1024)(128)(2,1)S(1)}) fusion(f32[768,1024]{1,0:T(8,128)} %get-tuple-element.18, f32[768]{0:T(1024)S(1)} %fusion.35, f32[768,1024]{1,0:T(8,128)} %get-tuple-element.17, bf16[768,1024]{1,0:T(8,128)(2,1)S(1)} %get-tuple-element.19, ...), kind=kOutput, calls=%fused_computation.21 | convolution fusion | flops 5643435008 | bytes 23859712 | tf_op jit(solution)/shard_map/dot_general | solution.py:8
  201.9 0.0 copy-start.5
  201.9 4.0 %fusion.20 = f32[768,1024]{1,0:T(8,128)S(1)} fusion(bf16[768,1024]{1,0:T(8,128)(2,1)S(1)} %get-tuple-element.30, bf16[1,3584,1024]{2,1,0:T(8,128)(2,1)} %param.14), kind=kOutput, calls=%fused_computation.27 | convolution fusion | flops 1610612736 | bytes 6815744 | tf_op jit(solution)/shard_map/dot_general | solution.py:8
  205.9 0.0 copy-done.5
  205.9 9.0 %fusion.9 = f32[768,2560]{1,0:T(8,128)} fusion(bf16[768,1024]{1,0:T(8,128)(2,1)S(1)} %get-tuple-element.31, bf16[1,3584,1024]{2,1,0:T(8,128)(2,1)} %param.13), kind=kOutput, calls=%fused_computation.11 | convolution fusion | flops 4026531840 | bytes 14680064 | tf_op jit(solution)/shard_map/dot_general | solution.py:8
  214.9 3.5 %add_convert_fusion.1 = bf16[768,1024]{1,0:T(8,128)(2,1)S(1)} fusion(f32[768,1024]{1,0:T(8,128)S(1)} %fusion.20, bf16[768,1024]{1,0:T(8,128)(2,1)S(1)} %get-tuple-element.31, bf16[1,3584,1024]{2,1,0:T(8,128)(2,1)} %param.13), kind=kOutput, calls=%fused_computation.20 | convolution fusion | flops 1612185600 | bytes 8388608 | tf_op jit(solution)/shard_map/dot_general | solution.py:8
  218.4 2.1 reshape.158
  220.5 7.5 %all-to-all-start.2 = ((bf16[128,48,128]{2,1,0:T(8,128)(2,1)}), bf16[128,48,128]{2,1,0:T(8,128)(2,1)S(1)}, u32[]{:S(2)}, u32[]{:S(2)}) async-start(bf16[128,48,128]{2,1,0:T(8,128)(2,1)} %reshape.158), calls=%async_computation.2 | async-start | bytes 3145728 | tf_op jit(solution)/shard_map/all_to_all | solution.py:50
  228.0 0.7 convert_select_fusion
  228.6 0.2 reshape.163
  228.8 9.5 %add_convert_fusion = bf16[768,2560]{1,0:T(8,128)(2,1)S(1)} fusion(f32[768,2560]{1,0:T(8,128)} %fusion.9, bf16[768,1024]{1,0:T(8,128)(2,1)} %copy-done.5, bf16[1,3584,1024]{2,1,0:T(8,128)(2,1)} %param.14), kind=kOutput, calls=%fused_computation.2 | convolution fusion | flops 4030464000 | bytes 18612224 | tf_op jit(solution)/shard_map/dot_general | solution.py:8
  238.3 2.1 fusion.13
  240.4 8.3 %reshape.161 = bf16[128,126,128]{2,1,0:T(8,128)(2,1)} reshape(bf16[768,2688]{1,0:T(8,128)(2,1)} %fusion.13) | data formatting | bytes 8257536 | tf_op jit(solution)/shard_map/reshape | solution.py:49
  248.8 3.9 %all-to-all-done.2 = bf16[128,48,128]{2,1,0:T(8,128)(2,1)S(1)} async-done(((bf16[128,48,128]{2,1,0:T(8,128)(2,1)}), bf16[128,48,128]{2,1,0:T(8,128)(2,1)S(1)}, u32[]{:S(2)}, u32[]{:S(2)}) %all-to-all-start.2) | async-done | bytes 1572896 | tf_op jit(solution)/shard_map/all_to_all | solution.py:50
  252.6 6.4 %all-to-all-start.3 = ((bf16[128,126,128]{2,1,0:T(8,128)(2,1)}), bf16[128,126,128]{2,1,0:T(8,128)(2,1)}, u32[]{:S(2)}, u32[]{:S(2)}) async-start(bf16[128,126,128]{2,1,0:T(8,128)(2,1)} %reshape.161), calls=%async_computation.3 | async-start | bytes 8388608 | tf_op jit(solution)/shard_map/all_to_all | solution.py:50
  259.0 2.1 reshape.159
  261.1 1.8 convolution_convert_fusion
  263.0 48.7 %all-to-all-done.3 = bf16[128,126,128]{2,1,0:T(8,128)(2,1)} async-done(((bf16[128,126,128]{2,1,0:T(8,128)(2,1)}), bf16[128,126,128]{2,1,0:T(8,128)(2,1)}, u32[]{:S(2)}, u32[]{:S(2)}) %all-to-all-start.3) | async-done | bytes 4128800 | tf_op jit(solution)/shard_map/all_to_all | solution.py:50
  311.6 0.0 copy-start.1
  311.6 8.2 %reshape.162 = bf16[768,2688]{1,0:T(8,128)(2,1)} reshape(bf16[128,126,128]{2,1,0:T(8,128)(2,1)} %all-to-all-done.3) | data formatting | bytes 8257536 | tf_op jit(solution)/shard_map/reshape | solution.py:51
  319.8 2.8 fusion.16
  322.7 1.4 fusion.27
  324.1 0.1 convert_element_type.60
  324.2 0.7 copy.34
  324.9 1.0 pad_maximum_fusion
  325.8 0.0 copy-done.1
  (11 shorter events, 0.1 us)
Async XLA Ops:
  0.6 3.0 copy-start
  18.7 12.0 %copy-start.4 = (bf16[128,4]{0,1:T(4,128)(2,1)S(1)}, bf16[128,4]{0,1:T(4,128)(2,1)}, u32[]{:S(2)}) copy-start(bf16[128,4]{0,1:T(4,128)(2,1)} %param.12) | copy-start | bytes 3076
  18.7 12.2 %copy-start.3 = (bf16[128,3584]{1,0:T(8,128)(2,1)S(1)}, bf16[128,3584]{1,0:T(8,128)(2,1)}, u32[]{:S(2)}) copy-start(bf16[128,3584]{1,0:T(8,128)(2,1)} %param.10) | copy-start | bytes 2752516
  18.7 80.4 %all-to-all-start.1 = ((bf16[128,168,128]{2,1,0:T(8,128)(2,1)}), bf16[128,168,128]{2,1,0:T(8,128)(2,1)}, u32[]{:S(2)}, u32[]{:S(2)}) async-start(bf16[128,168,128]{2,1,0:T(8,128)(2,1)} %reshape.156), calls=%async_computation.1 | async-start | bytes 11010048 | tf_op jit(solution)/shard_map/all_to_all | solution.py:50
  99.1 78.3 %all-to-all-start = ((bf16[128,174,128]{2,1,0:T(8,128)(2,1)}), bf16[128,174,128]{2,1,0:T(8,128)(2,1)}, u32[]{:S(2)}, u32[]{:S(2)}) async-start(bf16[128,174,128]{2,1,0:T(8,128)(2,1)} %reshape.154), calls=%async_computation | async-start | bytes 11534336 | tf_op jit(solution)/shard_map/all_to_all | solution.py:50
  118.2 10.6 %copy-start.2 = (bf16[768,3584]{1,0:T(8,128)(2,1)S(1)}, bf16[768,3584]{1,0:T(8,128)(2,1)}, u32[]{:S(2)}) copy-start(bf16[768,3584]{1,0:T(8,128)(2,1)} %reshape.157) | copy-start | bytes 16515076
  201.9 4.0 %copy-start.5 = (bf16[768,1024]{1,0:T(8,128)(2,1)}, bf16[768,1024]{1,0:T(8,128)(2,1)S(1)}, u32[]{:S(2)}) copy-start(bf16[768,1024]{1,0:T(8,128)(2,1)S(1)} %get-tuple-element.30) | copy-start | bytes 4718596
  220.5 32.2 %all-to-all-start.2 = ((bf16[128,48,128]{2,1,0:T(8,128)(2,1)}), bf16[128,48,128]{2,1,0:T(8,128)(2,1)S(1)}, u32[]{:S(2)}, u32[]{:S(2)}) async-start(bf16[128,48,128]{2,1,0:T(8,128)(2,1)} %reshape.158), calls=%async_computation.2 | async-start | bytes 3145728 | tf_op jit(solution)/shard_map/all_to_all | solution.py:50
  252.6 59.0 %all-to-all-start.3 = ((bf16[128,126,128]{2,1,0:T(8,128)(2,1)}), bf16[128,126,128]{2,1,0:T(8,128)(2,1)}, u32[]{:S(2)}, u32[]{:S(2)}) async-start(bf16[128,126,128]{2,1,0:T(8,128)(2,1)} %reshape.161), calls=%async_computation.3 | async-start | bytes 8388608 | tf_op jit(solution)/shard_map/all_to_all | solution.py:50
  311.6 14.2 %copy-start.1 = (bf16[128,3584]{1,0:T(8,128)(2,1)S(1)}, bf16[128,3584]{1,0:T(8,128)(2,1)}, u32[]{:S(2)}) copy-start(bf16[128,3584]{1,0:T(8,128)(2,1)} %param.9) | copy-start | bytes 2752516
